TPU v7x, 32 devices: a whole 2x2x4 slice. The times are simulated.
32 devices in a mesh: ctx: 8 (over z, y), seq: 4 (over x, core).
Axes of the slice: x: 2, y: 2, z: 4, core: 2. Of those that a mesh axis runs over, the one named last changes fastest.
Arguments:
- queries: bfloat16 [32768, 2048], P(('ctx', 'seq')), may hold values from -6 to 6
- keys: bfloat16 [32768, 2048], P(('ctx', 'seq')), may hold values from -6 to 6
- values: bfloat16 [32768, 2048], P(('ctx', 'seq')), may hold values from -6 to 6
- mixing: float32 [10, 16, 32768], P(None, None, ('ctx', 'seq')), may hold values from 0 to 1, as said below
Outputs:
- attended: float32 [32768, 2048], P(('ctx', 'seq'))
Inputs may be any that keep to these rules, and one draw needn't show every extreme that they name: Every mixing weight is positive and at most 1.
All inputs are finite; a program needn't handle non-finite values.
Results may differ from a plain program's by a relative error of at most 0.0028.
Values sent between devices are 32-bit elements; how exact they have to be, the bound alone decides.
No kernel may reach another device: no remote copies, remote signals or barrier semaphores. Data moves between devices by JAX's collectives and lax.ppermute only.
A program may use at most 192 MiB of HBM per device.

v0:
```python
import functools

import numpy as np
import jax
import jax.numpy as jnp
from jax import lax
from jax.experimental import pallas as pl
from jax.experimental.pallas import tpu as pltpu
from jax.sharding import PartitionSpec as P

SPAN = 64
TQ = 256
CHUNKS = 4
LOCAL_GROUP = 2


def level_masks(block, level_count):
    pos = np.arange(block)
    span = pos // SPAN
    crossed = span[:, None] ^ span[None, :]
    level = np.zeros_like(crossed)
    for power_index in range(level_count - 1):
        level = level + (crossed >= 2**power_index)
    causal = pos[:, None] >= pos[None, :]
    inner = int(np.log2(block // SPAN)) + 1
    return np.stack(
        [((level == l) & causal).astype(np.float32) for l in range(inner)]
    )


def state_kernel(head_count, k_ref, v_ref, o_ref):
    @pl.when(pl.program_id(0) == 0)
    def _():
        o_ref[...] = jnp.zeros_like(o_ref)

    dk = o_ref.shape[1]
    dv = o_ref.shape[2]
    for h in range(head_count):
        o_ref[h] += lax.dot_general(
            k_ref[:, h * dk:(h + 1) * dk], v_ref[:, h * dv:(h + 1) * dv],
            (((0,), (0,)), ((), ())), preferred_element_type=jnp.float32,
        )


def own_state(keys, values, head_count):
    rows, width = keys.shape
    dk = width // head_count
    dv = values.shape[1] // head_count
    tr = min(rows, 512)
    return pl.pallas_call(
        functools.partial(state_kernel, head_count),
        grid=(rows // tr,),
        in_specs=[
            pl.BlockSpec((tr, width), lambda r: (r, 0)),
            pl.BlockSpec((tr, values.shape[1]), lambda r: (r, 0)),
        ],
        out_specs=pl.BlockSpec((head_count, dk, dv), lambda r: (0, 0, 0)),
        out_shape=jax.ShapeDtypeStruct((head_count, dk, dv), jnp.float32),
        cost_estimate=pl.CostEstimate(
            flops=2 * rows * dk * dv * head_count,
            bytes_accessed=2 * rows * (dk + dv) * head_count + 4 * dk * dv * head_count,
            transcendentals=0,
        ),
        compiler_params=pltpu.CompilerParams(vmem_limit_bytes=64 * 1024 * 1024),
    )(keys, values)


def local_kernel(scale, rows, group, q_ref, k_ref, v_ref, m_ref, c_ref, *rest):
    o_ref = rest[-1]
    blocks = rows // TQ
    inner = c_ref.shape[0]
    dk = q_ref.shape[1] // group
    dv = v_ref.shape[1] // group
    for j in range(group):
        qc = slice(j * dk, (j + 1) * dk)
        vc = slice(j * dv, (j + 1) * dv)
        for a in range(blocks):
            r0 = a * TQ
            s = lax.dot_general(
                q_ref[r0:r0 + TQ, qc], k_ref[0:r0 + TQ, qc],
                (((1,), (1,)), ((), ())), preferred_element_type=jnp.float32,
            )
            s = s * scale
            mix = m_ref[j, r0:r0 + TQ, :]
            pieces = []
            for b in range(a):
                level = inner + (a ^ b).bit_length() - 1
                w = mix[:, level:level + 1]
                pieces.append((s[:, b * TQ:(b + 1) * TQ] * w).astype(jnp.bfloat16))
            wd = c_ref[0] * mix[:, 0:1]
            for l in range(1, inner):
                wd = wd + c_ref[l] * mix[:, l:l + 1]
            pieces.append((s[:, r0:r0 + TQ] * wd).astype(jnp.bfloat16))
            p = pieces[0] if len(pieces) == 1 else jnp.concatenate(pieces, axis=1)
            o_ref[r0:r0 + TQ, vc] = jnp.dot(
                p, v_ref[0:r0 + TQ, vc], preferred_element_type=jnp.float32
            )


def local_part(queries, keys, values, mix_t, masks, first, count, group, scale, prev):
    rows = queries.shape[0]
    head_count = mix_t.shape[0]
    dk = queries.shape[1] // head_count
    dv = values.shape[1] // head_count
    levels = mix_t.shape[2]
    blocks = rows // TQ
    tiles = blocks * (blocks + 1) // 2
    base = first // group
    in_specs = [
        pl.BlockSpec((rows, dk * group), lambda h: (0, h + base)),
        pl.BlockSpec((rows, dk * group), lambda h: (0, h + base)),
        pl.BlockSpec((rows, dv * group), lambda h: (0, h + base)),
        pl.BlockSpec((group, rows, levels), lambda h: (h + base, 0, 0)),
        pl.BlockSpec(masks.shape, lambda h: (0, 0, 0)),
    ]
    operands = [queries, keys, values, mix_t, masks]
    aliases = {}
    if prev is not None:
        in_specs.append(pl.BlockSpec(memory_space=pl.ANY))
        operands.append(prev)
        aliases = {5: 0}
    return pl.pallas_call(
        functools.partial(local_kernel, scale, rows, group),
        grid=(count // group,),
        in_specs=in_specs,
        out_specs=pl.BlockSpec((rows, dv * group), lambda h: (0, h + base)),
        out_shape=jax.ShapeDtypeStruct((rows, dv * head_count), jnp.float32),
        input_output_aliases=aliases,
        cost_estimate=pl.CostEstimate(
            flops=2 * tiles * TQ * TQ * (dk + dv) * count,
            bytes_accessed=(2 * rows * (2 * dk + dv) + 4 * rows * dv) * count,
            transcendentals=0,
        ),
        compiler_params=pltpu.CompilerParams(vmem_limit_bytes=64 * 1024 * 1024),
    )(*operands)


def cross_kernel(scale, rows, first_level, group, n_seq, n_ctx, sp_ref, q_ref, m_ref, l_ref, *rest):
    o_ref = rest[-1]
    seq_refs = rest[:n_seq]
    ctx_refs = rest[n_seq:n_seq + n_ctx]
    bits = n_seq + n_ctx
    dk = q_ref.shape[1] // group
    dv = l_ref.shape[1] // group
    for j in range(group):
        blocks = [seq_refs[b][j] for b in range(n_seq)]
        blocks += [ctx_refs[c][0, j] for c in range(n_ctx)]
        sib = jnp.concatenate(
            [
                (sp_ref[1 + b].astype(jnp.float32) * blocks[b]).astype(jnp.bfloat16)
                for b in range(bits)
            ],
            axis=1,
        )
        for a in range(rows // TQ):
            r0 = a * TQ
            t = jnp.dot(
                q_ref[r0:r0 + TQ, j * dk:(j + 1) * dk], sib,
                preferred_element_type=jnp.float32,
            )
            w_all = m_ref[j, r0:r0 + TQ, first_level:first_level + bits] * scale
            cross = w_all[:, 0:1] * t[:, 0:dv]
            for b in range(1, bits):
                cross = cross + w_all[:, b:b + 1] * t[:, b * dv:(b + 1) * dv]
            o_ref[r0:r0 + TQ, j * dv:(j + 1) * dv] = (
                l_ref[r0:r0 + TQ, j * dv:(j + 1) * dv] + cross
            )


def cross_all(queries, scalars, seq_sibs, ctx_stacks, mix_t, local, scale, first_level, group):
    rows = queries.shape[0]
    head_count = mix_t.shape[0]
    dk = queries.shape[1] // head_count
    levels = mix_t.shape[2]
    dv = local.shape[1] // head_count
    n_seq = len(seq_sibs)
    n_ctx = len(ctx_stacks)
    bits = n_seq + n_ctx
    in_specs = [
        pl.BlockSpec((rows, dk * group), lambda g, sp: (0, g)),
        pl.BlockSpec((group, rows, levels), lambda g, sp: (g, 0, 0)),
        pl.BlockSpec((rows, dv * group), lambda g, sp: (0, g)),
    ]
    for x in seq_sibs:
        in_specs.append(pl.BlockSpec((group, dk, dv), lambda g, sp: (g, 0, 0)))
    for x in ctx_stacks:
        in_specs.append(
            pl.BlockSpec((1, group, dk, dv), lambda g, sp: (jnp.bitwise_xor(sp[0], g), 0, 0, 0))
        )
    return pl.pallas_call(
        functools.partial(cross_kernel, scale, rows, first_level, group, n_seq, n_ctx),
        grid_spec=pltpu.PrefetchScalarGridSpec(
            num_scalar_prefetch=1,
            grid=(head_count // group,),
            in_specs=in_specs,
            out_specs=pl.BlockSpec((rows, dv * group), lambda g, sp: (0, g)),
        ),
        out_shape=jax.ShapeDtypeStruct((rows, dv * head_count), jnp.float32),
        input_output_aliases={3: 0},
        cost_estimate=pl.CostEstimate(
            flops=2 * rows * dk * dv * bits * head_count,
            bytes_accessed=(2 * rows * dk + 8 * rows * dv) * head_count,
            transcendentals=0,
        ),
        compiler_params=pltpu.CompilerParams(vmem_limit_bytes=64 * 1024 * 1024),
    )(scalars, queries, mix_t, local, *seq_sibs, *ctx_stacks)


def swap(block, axis, bit, one_way=False):
    count = lax.axis_size(axis)
    route = []
    for low in range(count):
        high = low | 1 << bit
        if high != low and high < count:
            route.append((low, high))
            if not one_way:
                route.append((high, low))
    return lax.ppermute(block, axis, route)


def to_offset(block, axis, offset):
    count = lax.axis_size(axis)
    return lax.ppermute(block, axis, [(s, s ^ offset) for s in range(count)])


def shards(queries, keys, values, mixing):
    rows = queries.shape[0]
    head_count = mixing.shape[1]
    dk = queries.shape[1] // head_count
    scale = dk ** (-0.5)
    level_count = (rows // SPAN).bit_length()
    mix_t = mixing.transpose(1, 2, 0)
    masks = jnp.asarray(level_masks(TQ, level_count))

    state = own_state(keys, values, head_count)

    seq_count = lax.axis_size("seq")
    ctx_count = lax.axis_size("ctx")
    seq_bits = seq_count.bit_length() - 1
    ctx_bits = ctx_count.bit_length() - 1
    seq_place = lax.axis_index("seq")
    ctx_place = lax.axis_index("ctx")

    sibs = []
    flags = []
    running = state
    half = head_count // 2
    for bit in range(seq_bits):
        if bit == 0 or seq_count < 4:
            partner = swap(running, "seq", bit)
        else:
            mine = seq_place & 1
            sent = lax.dynamic_slice_in_dim(running, mine * half, half, 0)
            got = swap(sent, "seq", bit)
            other = swap(got, "seq", 0)
            lo = jnp.where(mine == 0, got, other)
            hi = jnp.where(mine == 0, other, got)
            partner = jnp.concatenate([lo, hi], axis=0)
        sibs.append(partner)
        flags.append(seq_place >> bit & 1)
        running = running + partner

    share = head_count // seq_count
    quarter = lax.dynamic_slice_in_dim(running, seq_place * share, share, 0)
    ctx_sibs = []
    for bit in range(ctx_bits):
        got = swap(quarter, "ctx", bit, one_way=(bit == ctx_bits - 1))
        ctx_sibs.append(got)
        if bit != ctx_bits - 1:
            quarter = quarter + got

    ctx_stacks = []
    for bit in range(ctx_bits):
        part = lax.optimization_barrier(ctx_sibs[bit])
        parts = {0: part}
        for offset in range(1, seq_count):
            if offset & 1 and offset > 1:
                parts[offset] = to_offset(parts[offset ^ 1], "seq", 1)
            else:
                parts[offset] = to_offset(part, "seq", offset)
        ctx_stacks.append(jnp.stack([parts[o] for o in range(seq_count)]))
        flags.append(ctx_place >> bit & 1)
    scalars = jnp.stack([seq_place] + flags).astype(jnp.int32)

    per = head_count // CHUNKS
    local = None
    for c in range(CHUNKS):
        local = local_part(
            queries, keys, values, mix_t, masks, c * per, per, LOCAL_GROUP, scale, local
        )
    return cross_all(
        queries, scalars, sibs, ctx_stacks, mix_t, local, scale, level_count,
        head_count // seq_count,
    )


def solution(mesh):
    return jax.shard_map(
        shards,
        mesh=mesh,
        in_specs=(
            P(("ctx", "seq"), None),
            P(("ctx", "seq"), None),
            P(("ctx", "seq"), None),
            P(None, None, ("ctx", "seq")),
        ),
        out_specs=P(("ctx", "seq"), None),
        check_vma=False,
    )
```

profile of v0, /device:TPU:0, one launch (start us, length us, event | category | flops | bytes accessed | tf_op | source)
XLA Modules:
  0.0 111.5 jit_solution(16662011077344561990)
XLA Ops:
  0.0 5.3 %shard_map.59 = f32[16,128,128]{2,1,0:T(8,128)} custom-call(bf16[1024,2048]{1,0:T(8,128)(2,1)} %k_ref.9, bf16[1024,2048]{1,0:T(8,128)(2,1)} %v_ref.9), custom_call_target="tpu_custom_call" | custom-call | flops 536870912 | bytes 9437184 | tf_op jit(solution)/shard_map/pallas_call | solution.py:50
  5.3 0.5 collective-permute-start
  5.7 2.5 %collective-permute-done.rest_0_ = f32[16,128,128]{2,1,0:T(8,128)S(1)} collective-permute-done((f32[16,128,128]{2,1,0:T(8,128)}, f32[16,128,128]{2,1,0:T(8,128)S(1)}, u32[]{:S(2)}, u32[]{:S(2)}) %collective-permute-start) | collective-permute-done | bytes 1048608 | tf_op jit(solution)/shard_map/ppermute | solution.py:218
  8.2 1.7 %add.18 = f32[16,128,128]{2,1,0:T(8,128)S(1)} add(f32[16,128,128]{2,1,0:T(8,128)} %shard_map.59, f32[16,128,128]{2,1,0:T(8,128)S(1)} %collective-permute-done.rest_0_) | non-fusion elementwise | flops 262144 | bytes 3145728 | tf_op jit(solution)/shard_map/add | solution.py:261
  10.0 2.9 %collective-permute-start.1 = (f32[8,128,128]{2,1,0:T(8,128)S(1)}, f32[8,128,128]{2,1,0:T(8,128)S(1)}, u32[]{:S(2)}, u32[]{:S(2)}) collective-permute-start(f32[8,128,128]{2,1,0:T(8,128)S(1)} %constant_dynamic-slice_fusion), channel_id=1, source_target_pairs={{0,2},{2,0},{1,3},{3,1},{4,6},{6,4},{5,7},{7,5},{8,10},{10,8},{9,1... | collective-permute-start | bytes 1572872 | tf_op jit(solution)/shard_map/ppermute | solution.py:218
  12.9 12.2 %collective-permute-done.1 = f32[8,128,128]{2,1,0:T(8,128)S(1)} collective-permute-done((f32[8,128,128]{2,1,0:T(8,128)S(1)}, f32[8,128,128]{2,1,0:T(8,128)S(1)}, u32[]{:S(2)}, u32[]{:S(2)}) %collective-permute-start.1) | collective-permute-done | bytes 524320 | tf_op jit(solution)/shard_map/ppermute | solution.py:218
  25.2 0.0 collective-permute-start.2
  25.2 2.0 %collective-permute-done.2 = f32[8,128,128]{2,1,0:T(8,128)} collective-permute-done((f32[8,128,128]{2,1,0:T(8,128)S(1)}, f32[8,128,128]{2,1,0:T(8,128)}, u32[]{:S(2)}, u32[]{:S(2)}) %collective-permute-start.2) | collective-permute-done | bytes 524320 | tf_op jit(solution)/shard_map/ppermute | solution.py:218
  27.2 1.1 %broadcast_select_fusion.1 = (f32[8,128,128]{2,1,0:T(8,128)S(1)}, f32[8,128,128]{2,1,0:T(8,128)S(1)}) fusion(f32[8,128,128]{2,1,0:T(8,128)S(1)} %collective-permute-done.1, f32[8,128,128]{2,1,0:T(8,128)} %collective-permute-done.2, pred[]{:T(512)S(6)} %eq.4), kind=kLoop, calls=%fused_computation.9 | loop fusion | flops 262144 | bytes 2097153 | tf_op jit(solution)/shard_map/jit(_where)/select_n | solution.py:256
  28.4 0.8 copy-done
  29.1 0.1 fusion.1
  29.2 0.1 copy-done.1
  29.3 1.8 %collective-permute-start.3 = (f32[4,128,128]{2,1,0:T(8,128)S(1)}, f32[4,128,128]{2,1,0:T(8,128)}, u32[]{:S(2)}, u32[]{:S(2)}) collective-permute-start(f32[4,128,128]{2,1,0:T(8,128)S(1)} %fusion.1), channel_id=1, source_target_pairs={{0,4},{4,0},{8,12},{12,8},{16,20},{20,16},{24,28},{28,24},{1,5},{5... | collective-permute-start | bytes 786440 | tf_op jit(solution)/shard_map/ppermute | solution.py:218
  31.1 6.7 %collective-permute-done.3 = f32[4,128,128]{2,1,0:T(8,128)} collective-permute-done((f32[4,128,128]{2,1,0:T(8,128)S(1)}, f32[4,128,128]{2,1,0:T(8,128)}, u32[]{:S(2)}, u32[]{:S(2)}) %collective-permute-start.3) | collective-permute-done | bytes 262176 | tf_op jit(solution)/shard_map/ppermute | solution.py:218
  37.8 1.0 add.22
  38.8 1.9 %collective-permute-start.7 = (f32[4,128,128]{2,1,0:T(8,128)S(1)}, f32[4,128,128]{2,1,0:T(8,128)S(1)}, u32[]{:S(2)}, u32[]{:S(2)}) collective-permute-start(f32[4,128,128]{2,1,0:T(8,128)S(1)} %add.22), channel_id=1, source_target_pairs={{0,8},{8,0},{4,12},{12,4},{16,24},{24,16},{20,28},{28,20},{1,9},{9... | collective-permute-start | bytes 786440 | tf_op jit(solution)/shard_map/ppermute | solution.py:218
  40.7 4.7 %copy.10 = f32[10,16,1024]{0,2,1:T(8,128)} copy(f32[10,16,1024]{2,1,0:T(8,128)S(1)} %copy-done.4) | data formatting | bytes 1310720 | tf_op args[3]
  45.4 1.5 %collective-permute-start.5 = (f32[4,128,128]{2,1,0:T(8,128)}, f32[4,128,128]{2,1,0:T(8,128)}, u32[]{:S(2)}, u32[]{:S(2)}) collective-permute-start(f32[4,128,128]{2,1,0:T(8,128)} %collective-permute-done.3), channel_id=1, source_target_pairs={{0,2},{1,3},{2,0},{3,1},{4,6},{5,7},{6,4},{7,5},{8,10},{9,11},{10,... | collective-permute-start | bytes 786440 | tf_op jit(solution)/shard_map/ppermute | solution.py:223
  46.9 0.0 collective-permute-done.7
  46.9 0.8 add.23
  47.7 0.0 copy-done.3
  47.7 5.2 %collective-permute-start.11 = (f32[4,128,128]{2,1,0:T(8,128)}, f32[4,128,128]{2,1,0:T(8,128)}, u32[]{:S(2)}, u32[]{:S(2)}) collective-permute-start(f32[4,128,128]{2,1,0:T(8,128)} %add.23), channel_id=1, source_target_pairs={{0,16},{4,20},{8,24},{12,28},{1,17},{5,21},{9,25},{13,29},{2,18},{... | collective-permute-start | bytes 786440 | tf_op jit(solution)/shard_map/ppermute | solution.py:218
  52.9 7.1 %shard_map.55.rest_0_ = f32[1024,2048]{1,0:T(8,128)} custom-call(bf16[1024,2048]{1,0:T(8,128)(2,1)} %q_ref.9, bf16[1024,2048]{1,0:T(8,128)(2,1)} %k_ref.9, bf16[1024,2048]{1,0:T(8,128)(2,1)} %v_ref.9, f32[16,1024,10]{2,1,0:T(8,128)} %bitcast.19, f32[3,256,256]{2,1,0:T(8,128)} %constant.23.clone.c_ref), custom_call_target="tpu_custom_call" | custom-call | flops 1342177280 | bytes 5242880 | tf_op jit(solution)/shard_map/pallas_call | solution.py:122
  60.0 1.2 %collective-permute-start.9 = (f32[4,128,128]{2,1,0:T(8,128)}, f32[4,128,128]{2,1,0:T(8,128)}, u32[]{:S(2)}, u32[]{:S(2)}) collective-permute-start(f32[4,128,128]{2,1,0:T(8,128)} %copy-done.3), channel_id=1, source_target_pairs={{0,2},{1,3},{2,0},{3,1},{4,6},{5,7},{6,4},{7,5},{8,10},{9,11},{10,... | collective-permute-start | bytes 786440 | tf_op jit(solution)/shard_map/ppermute | solution.py:223
  61.2 7.0 %shard_map.56.rest_0_ = f32[1024,2048]{1,0:T(8,128)} custom-call(bf16[1024,2048]{1,0:T(8,128)(2,1)} %q_ref.9, bf16[1024,2048]{1,0:T(8,128)(2,1)} %k_ref.9, bf16[1024,2048]{1,0:T(8,128)(2,1)} %v_ref.9, f32[16,1024,10]{2,1,0:T(8,128)} %bitcast.20, f32[3,256,256]{2,1,0:T(8,128)} %constant.23.clone.c_ref, ...), custom_call_target="tpu_custom_call", output_to_operand_aliasing={{}: (5, {})} | custom-call | flops 1342177280 | bytes 5242880 | tf_op jit(solution)/shard_map/pallas_call | solution.py:122
  68.2 0.7 stack.72.sp_ref
  68.8 7.0 %shard_map.57.rest_0_ = f32[1024,2048]{1,0:T(8,128)} custom-call(bf16[1024,2048]{1,0:T(8,128)(2,1)} %q_ref.9, bf16[1024,2048]{1,0:T(8,128)(2,1)} %k_ref.9, bf16[1024,2048]{1,0:T(8,128)(2,1)} %v_ref.9, f32[16,1024,10]{2,1,0:T(8,128)} %bitcast.21, f32[3,256,256]{2,1,0:T(8,128)} %constant.23.clone.c_ref, ...), custom_call_target="tpu_custom_call", output_to_operand_aliasing={{}: (5, {})} | custom-call | flops 1342177280 | bytes 5242880 | tf_op jit(solution)/shard_map/pallas_call | solution.py:122
  75.8 0.0 collective-permute-start.4
  75.8 0.0 collective-permute-done.5
  75.8 0.5 collective-permute-start.6
  76.3 0.0 collective-permute-done.11
  76.3 0.8 collective-permute-start.13
  77.2 7.0 %shard_map.58.l_ref = f32[1024,2048]{1,0:T(8,128)} custom-call(bf16[1024,2048]{1,0:T(8,128)(2,1)} %q_ref.9, bf16[1024,2048]{1,0:T(8,128)(2,1)} %k_ref.9, bf16[1024,2048]{1,0:T(8,128)(2,1)} %v_ref.9, f32[16,1024,10]{2,1,0:T(8,128)} %bitcast.22, f32[3,256,256]{2,1,0:T(8,128)} %constant.23.clone.c_ref, ...), custom_call_target="tpu_custom_call", output_to_operand_aliasing={{}: (5, {})} | custom-call | flops 1342177280 | bytes 5242880 | tf_op jit(solution)/shard_map/pallas_call | solution.py:122
  84.1 0.0 collective-permute-start.8
  84.1 0.0 collective-permute-done.9
  84.1 0.5 collective-permute-start.10
  84.6 2.3 %pad_maximum_fusion.rest_1_ = f32[16,128,128]{2,1,0:T(8,128)} fusion(f32[8,128,128]{2,1,0:T(8,128)} %copy-done.1, f32[8,128,128]{2,1,0:T(8,128)} %copy-done), kind=kLoop, calls=%fused_computation.1 | loop fusion | flops 262144 | bytes 2097152 | tf_op jit(solution)/shard_map/concatenate | solution.py:258
  86.9 0.0 collective-permute-done.4
  86.9 0.1 collective-permute-start.12
  87.0 0.0 collective-permute-done.13
  87.0 0.4 collective-permute-start.14
  87.4 0.0 collective-permute-done.6
  87.4 2.3 %pad_maximum_fusion.1.rest_2_ = f32[4,4,128,128]{3,2,1,0:T(8,128)} fusion(f32[1,4,128,128]{3,2,1,0:T(8,128)} %bitcast.10, f32[1,4,128,128]{3,2,1,0:T(8,128)} %bitcast.9, f32[1,4,128,128]{3,2,1,0:T(8,128)} %bitcast.8, f32[1,4,128,128]{3,2,1,0:T(8,128)} %bitcast.7), kind=kLoop, calls=%fused_computation.3 | loop fusion | flops 786432 | bytes 2097152 | tf_op jit(solution)/shard_map/stack | solution.py:281
  89.7 2.1 %pad_maximum_fusion.2.rest_3_ = f32[4,4,128,128]{3,2,1,0:T(8,128)} fusion(f32[1,4,128,128]{3,2,1,0:T(8,128)S(1)} %bitcast.26, f32[1,4,128,128]{3,2,1,0:T(8,128)} %bitcast.13, f32[1,4,128,128]{3,2,1,0:T(8,128)S(1)} %bitcast.25, f32[1,4,128,128]{3,2,1,0:T(8,128)} %bitcast.24), kind=kLoop, calls=%fused_computation.4 | loop fusion | flops 786432 | bytes 2097152 | tf_op jit(solution)/shard_map/stack | solution.py:281
  91.8 0.0 collective-permute-done.12
  91.8 0.0 collective-permute-done.14
  91.8 2.2 %pad_maximum_fusion.3.rest_4_ = f32[4,4,128,128]{3,2,1,0:T(8,128)} fusion(f32[1,4,128,128]{3,2,1,0:T(8,128)S(1)} %bitcast.28, f32[1,4,128,128]{3,2,1,0:T(8,128)} %bitcast.17, f32[1,4,128,128]{3,2,1,0:T(8,128)S(1)} %bitcast.27, f32[1,4,128,128]{3,2,1,0:T(8,128)} %bitcast.15), kind=kLoop, calls=%fused_computation.5 | loop fusion | flops 786432 | bytes 2097152 | tf_op jit(solution)/shard_map/stack | solution.py:281
  94.0 17.6 %shard_map.60 = f32[1024,2048]{1,0:T(8,128)} custom-call(s32[6]{0:T(128)} %stack.72.sp_ref, bf16[1024,2048]{1,0:T(8,128)(2,1)} %q_ref.9, f32[16,1024,10]{2,1,0:T(8,128)} %bitcast.23, f32[1024,2048]{1,0:T(8,128)} %shard_map.58.l_ref, f32[16,128,128]{2,1,0:T(8,128)} %copy-done.2, ...), custom_call_target="tpu_custom_call", output_to_operand_aliasing={{}: (3, {})} | custom-call | flops 2684354560 | bytes 20971520 | tf_op jit(solution)/shard_map/pallas_call | solution.py:190
  (10 shorter events, 0.1 us)
Async XLA Ops:
  5.3 35.4 %copy-start.4 = (f32[10,16,1024]{2,1,0:T(8,128)S(1)}, f32[10,16,1024]{2,1,0:T(8,128)}, u32[]{:S(2)}) copy-start(f32[10,16,1024]{2,1,0:T(8,128)} %param.8) | copy-start | bytes 1966084
  5.3 3.0 %collective-permute-start = (f32[16,128,128]{2,1,0:T(8,128)}, f32[16,128,128]{2,1,0:T(8,128)S(1)}, u32[]{:S(2)}, u32[]{:S(2)}) collective-permute-start(f32[16,128,128]{2,1,0:T(8,128)} %shard_map.59), channel_id=1, source_target_pairs={{0,1},{1,0},{2,3},{3,2},{4,5},{5,4},{6,7},{7,6},{8,9},{9,8},{10,11... | collective-permute-start | bytes 3145736 | tf_op jit(solution)/shard_map/ppermute | solution.py:218
  8.2 37.1 %copy-start.2 = (f32[16,128,128]{2,1,0:T(8,128)}, f32[16,128,128]{2,1,0:T(8,128)S(1)}, u32[]{:S(2)}) copy-start(f32[16,128,128]{2,1,0:T(8,128)S(1)} %collective-permute-done.rest_0_) | copy-start | bytes 3145732
  10.0 15.1 %collective-permute-start.1 = (f32[8,128,128]{2,1,0:T(8,128)S(1)}, f32[8,128,128]{2,1,0:T(8,128)S(1)}, u32[]{:S(2)}, u32[]{:S(2)}) collective-permute-start(f32[8,128,128]{2,1,0:T(8,128)S(1)} %constant_dynamic-slice_fusion), channel_id=1, source_target_pairs={{0,2},{2,0},{1,3},{3,1},{4,6},{6,4},{5,7},{7,5},{8,10},{10,8},{9,1... | collective-permute-start | bytes 1572872 | tf_op jit(solution)/shard_map/ppermute | solution.py:218
  25.2 2.0 %collective-permute-start.2 = (f32[8,128,128]{2,1,0:T(8,128)S(1)}, f32[8,128,128]{2,1,0:T(8,128)}, u32[]{:S(2)}, u32[]{:S(2)}) collective-permute-start(f32[8,128,128]{2,1,0:T(8,128)S(1)} %collective-permute-done.1), channel_id=1, source_target_pairs={{0,1},{1,0},{2,3},{3,2},{4,5},{5,4},{6,7},{7,6},{8,9},{9,8},{10,11... | collective-permute-start | bytes 1572872 | tf_op jit(solution)/shard_map/ppermute | solution.py:218
  28.3 0.8 copy-start
  28.3 1.0 copy-start.1
  29.3 8.5 %collective-permute-start.3 = (f32[4,128,128]{2,1,0:T(8,128)S(1)}, f32[4,128,128]{2,1,0:T(8,128)}, u32[]{:S(2)}, u32[]{:S(2)}) collective-permute-start(f32[4,128,128]{2,1,0:T(8,128)S(1)} %fusion.1), channel_id=1, source_target_pairs={{0,4},{4,0},{8,12},{12,8},{16,20},{20,16},{24,28},{28,24},{1,5},{5... | collective-permute-start | bytes 786440 | tf_op jit(solution)/shard_map/ppermute | solution.py:218
  38.8 8.1 %collective-permute-start.7 = (f32[4,128,128]{2,1,0:T(8,128)S(1)}, f32[4,128,128]{2,1,0:T(8,128)S(1)}, u32[]{:S(2)}, u32[]{:S(2)}) collective-permute-start(f32[4,128,128]{2,1,0:T(8,128)S(1)} %add.22), channel_id=1, source_target_pairs={{0,8},{8,0},{4,12},{12,4},{16,24},{24,16},{20,28},{28,20},{1,9},{9... | collective-permute-start | bytes 786440 | tf_op jit(solution)/shard_map/ppermute | solution.py:218
  45.4 30.4 %collective-permute-start.5 = (f32[4,128,128]{2,1,0:T(8,128)}, f32[4,128,128]{2,1,0:T(8,128)}, u32[]{:S(2)}, u32[]{:S(2)}) collective-permute-start(f32[4,128,128]{2,1,0:T(8,128)} %collective-permute-done.3), channel_id=1, source_target_pairs={{0,2},{1,3},{2,0},{3,1},{4,6},{5,7},{6,4},{7,5},{8,10},{9,11},{10,... | collective-permute-start | bytes 786440 | tf_op jit(solution)/shard_map/ppermute | solution.py:223
  46.9 0.8 copy-start.3
  47.7 28.6 %collective-permute-start.11 = (f32[4,128,128]{2,1,0:T(8,128)}, f32[4,128,128]{2,1,0:T(8,128)}, u32[]{:S(2)}, u32[]{:S(2)}) collective-permute-start(f32[4,128,128]{2,1,0:T(8,128)} %add.23), channel_id=1, source_target_pairs={{0,16},{4,20},{8,24},{12,28},{1,17},{5,21},{9,25},{13,29},{2,18},{... | collective-permute-start | bytes 786440 | tf_op jit(solution)/shard_map/ppermute | solution.py:218
  60.0 24.1 %collective-permute-start.9 = (f32[4,128,128]{2,1,0:T(8,128)}, f32[4,128,128]{2,1,0:T(8,128)}, u32[]{:S(2)}, u32[]{:S(2)}) collective-permute-start(f32[4,128,128]{2,1,0:T(8,128)} %copy-done.3), channel_id=1, source_target_pairs={{0,2},{1,3},{2,0},{3,1},{4,6},{5,7},{6,4},{7,5},{8,10},{9,11},{10,... | collective-permute-start | bytes 786440 | tf_op jit(solution)/shard_map/ppermute | solution.py:223
  75.8 11.1 %collective-permute-start.4 = (f32[4,128,128]{2,1,0:T(8,128)}, f32[4,128,128]{2,1,0:T(8,128)}, u32[]{:S(2)}, u32[]{:S(2)}) collective-permute-start(f32[4,128,128]{2,1,0:T(8,128)} %collective-permute-done.3), channel_id=1, source_target_pairs={{0,1},{1,0},{2,3},{3,2},{4,5},{5,4},{6,7},{7,6},{8,9},{9,8},{10,11... | collective-permute-start | bytes 786440 | tf_op jit(solution)/shard_map/ppermute | solution.py:223
  75.8 11.6 %collective-permute-start.6 = (f32[4,128,128]{2,1,0:T(8,128)}, f32[4,128,128]{2,1,0:T(8,128)}, u32[]{:S(2)}, u32[]{:S(2)}) collective-permute-start(f32[4,128,128]{2,1,0:T(8,128)} %collective-permute-done.5), channel_id=1, source_target_pairs={{0,1},{1,0},{2,3},{3,2},{4,5},{5,4},{6,7},{7,6},{8,9},{9,8},{10,11... | collective-permute-start | bytes 786440 | tf_op jit(solution)/shard_map/ppermute | solution.py:223
  76.3 10.7 %collective-permute-start.13 = (f32[4,128,128]{2,1,0:T(8,128)}, f32[4,128,128]{2,1,0:T(8,128)}, u32[]{:S(2)}, u32[]{:S(2)}) collective-permute-start(f32[4,128,128]{2,1,0:T(8,128)} %collective-permute-done.11), channel_id=1, source_target_pairs={{0,2},{1,3},{2,0},{3,1},{4,6},{5,7},{6,4},{7,5},{8,10},{9,11},{10,... | collective-permute-start | bytes 786440 | tf_op jit(solution)/shard_map/ppermute | solution.py:223
  84.1 5.6 %collective-permute-start.8 = (f32[4,128,128]{2,1,0:T(8,128)}, f32[4,128,128]{2,1,0:T(8,128)S(1)}, u32[]{:S(2)}, u32[]{:S(2)}) collective-permute-start(f32[4,128,128]{2,1,0:T(8,128)} %copy-done.3), channel_id=1, source_target_pairs={{0,1},{1,0},{2,3},{3,2},{4,5},{5,4},{6,7},{7,6},{8,9},{9,8},{10,11... | collective-permute-start | bytes 786440 | tf_op jit(solution)/shard_map/ppermute | solution.py:223
  84.1 5.6 %collective-permute-start.10 = (f32[4,128,128]{2,1,0:T(8,128)}, f32[4,128,128]{2,1,0:T(8,128)S(1)}, u32[]{:S(2)}, u32[]{:S(2)}) collective-permute-start(f32[4,128,128]{2,1,0:T(8,128)} %collective-permute-done.9), channel_id=1, source_target_pairs={{0,1},{1,0},{2,3},{3,2},{4,5},{5,4},{6,7},{7,6},{8,9},{9,8},{10,11... | collective-permute-start | bytes 786440 | tf_op jit(solution)/shard_map/ppermute | solution.py:223
  86.9 4.9 %collective-permute-start.12 = (f32[4,128,128]{2,1,0:T(8,128)}, f32[4,128,128]{2,1,0:T(8,128)S(1)}, u32[]{:S(2)}, u32[]{:S(2)}) collective-permute-start(f32[4,128,128]{2,1,0:T(8,128)} %collective-permute-done.11), channel_id=1, source_target_pairs={{0,1},{1,0},{2,3},{3,2},{4,5},{5,4},{6,7},{7,6},{8,9},{9,8},{10,11... | collective-permute-start | bytes 786440 | tf_op jit(solution)/shard_map/ppermute | solution.py:223
  87.0 4.8 %collective-permute-start.14 = (f32[4,128,128]{2,1,0:T(8,128)}, f32[4,128,128]{2,1,0:T(8,128)S(1)}, u32[]{:S(2)}, u32[]{:S(2)}) collective-permute-start(f32[4,128,128]{2,1,0:T(8,128)} %collective-permute-done.13), channel_id=1, source_target_pairs={{0,1},{1,0},{2,3},{3,2},{4,5},{5,4},{6,7},{7,6},{8,9},{9,8},{10,11... | collective-permute-start | bytes 786440 | tf_op jit(solution)/shard_map/ppermute | solution.py:223
where the time goes:
time: 112 us
  Pallas kernels  50.8 us (45%)
  waiting for transfers between devices  23.5 us (21%)
  starting transfers between devices  17.3 us (15%)
  other arithmetic  13.5 us (12%)
  local copies, waits for them, and re-layouts  6.37 us (6%)
    pallas_call x4, Pallas kernels, local_part(): pl.pallas_call(functools.partial(local_kernel, scale, rows, group), grid=...  28 us
    ppermute x6, waiting for transfers between devices, swap(): return lax.ppermute(block, axis, route)  23.5 us
    pallas_call x1, Pallas kernels, cross_all(): pl.pallas_call(functools.partial(cross_kernel, scale, rows, first_level,...  17.6 us
    ppermute x6, starting transfers between devices, swap(): return lax.ppermute(block, axis, route)  12.2 us
    another operation x3, other arithmetic, shards(): ctx_stacks.append(jnp.stack([parts[o] for o in range(seq_count)]))  6.53 us
    unnamed x11, local copies, waits for them, and re-layouts  5.65 us
    pallas_call x1, Pallas kernels, own_state(): pl.pallas_call(functools.partial(state_kernel, head_count), grid=(rows //...  5.25 us
    ppermute x9, starting transfers between devices, to_offset(): return lax.ppermute(block, axis, [(s, s ^ offset) for s in range(count)])  5.04 us
  transfers between devices with their start and end apart: 15, of which 4 were waited for; matrix products, arithmetic and copies ran while one was open for 12% of the time, Pallas kernels for 25%

commit v1 on v0

--- a/solution.py
+++ b/solution.py
@@ -135,15 +135,28 @@
     )(*operands)
 
 
-def cross_kernel(scale, rows, first_level, group, n_seq, n_ctx, sp_ref, q_ref, m_ref, l_ref, *rest):
+def cross_kernel(scale, rows, first_level, group, kinds, halves, sp_ref, q_ref, m_ref, l_ref, *rest):
     o_ref = rest[-1]
-    seq_refs = rest[:n_seq]
-    ctx_refs = rest[n_seq:n_seq + n_ctx]
+    n_seq = len(kinds)
+    seq_refs = []
+    at = 0
+    for two in kinds:
+        seq_refs.append((rest[at], rest[at + 1]) if two else rest[at])
+        at += 2 if two else 1
+    n_ctx = len(rest) - 1 - at
+    ctx_refs = rest[at:at + n_ctx]
     bits = n_seq + n_ctx
     dk = q_ref.shape[1] // group
     dv = l_ref.shape[1] // group
     for j in range(group):
-        blocks = [seq_refs[b][j] for b in range(n_seq)]
+        blocks = []
+        for b in range(n_seq):
+            if isinstance(seq_refs[b], tuple):
+                got_ref, other_ref = seq_refs[b]
+                use_got = pl.program_id(0) // halves == jnp.bitwise_and(sp_ref[0], 1)
+                blocks.append(jnp.where(use_got, got_ref[j], other_ref[j]))
+            else:
+                blocks.append(seq_refs[b][j])
         blocks += [ctx_refs[c][0, j] for c in range(n_ctx)]
         sib = jnp.concatenate(
             [
@@ -181,14 +194,25 @@
         pl.BlockSpec((group, rows, levels), lambda g, sp: (g, 0, 0)),
         pl.BlockSpec((rows, dv * group), lambda g, sp: (0, g)),
     ]
+    kinds = []
+    flat = []
+    halves = head_count // 2 // group
     for x in seq_sibs:
-        in_specs.append(pl.BlockSpec((group, dk, dv), lambda g, sp: (g, 0, 0)))
+        if isinstance(x, tuple):
+            kinds.append(True)
+            for y in x:
+                in_specs.append(pl.BlockSpec((group, dk, dv), lambda g, sp: (g % halves, 0, 0)))
+                flat.append(y)
+        else:
+            kinds.append(False)
+            in_specs.append(pl.BlockSpec((group, dk, dv), lambda g, sp: (g, 0, 0)))
+            flat.append(x)
     for x in ctx_stacks:
         in_specs.append(
             pl.BlockSpec((1, group, dk, dv), lambda g, sp: (jnp.bitwise_xor(sp[0], g), 0, 0, 0))
         )
     return pl.pallas_call(
-        functools.partial(cross_kernel, scale, rows, first_level, group, n_seq, n_ctx),
+        functools.partial(cross_kernel, scale, rows, first_level, group, tuple(kinds), halves),
         grid_spec=pltpu.PrefetchScalarGridSpec(
             num_scalar_prefetch=1,
             grid=(head_count // group,),
@@ -203,7 +227,7 @@
             transcendentals=0,
         ),
         compiler_params=pltpu.CompilerParams(vmem_limit_bytes=64 * 1024 * 1024),
-    )(scalars, queries, mix_t, local, *seq_sibs, *ctx_stacks)
+    )(scalars, queries, mix_t, local, *flat, *ctx_stacks)
 
 
 def swap(block, axis, bit, one_way=False):
@@ -248,6 +272,7 @@
     for bit in range(seq_bits):
         if bit == 0 or seq_count < 4:
             partner = swap(running, "seq", bit)
+            sibs.append(partner)
         else:
             mine = seq_place & 1
             sent = lax.dynamic_slice_in_dim(running, mine * half, half, 0)
@@ -256,7 +281,7 @@
             lo = jnp.where(mine == 0, got, other)
             hi = jnp.where(mine == 0, other, got)
             partner = jnp.concatenate([lo, hi], axis=0)
-        sibs.append(partner)
+            sibs.append((got, other))
         flags.append(seq_place >> bit & 1)
         running = running + partner
 

time: 112 us -> 115 us (1.027)
  waiting for transfers between devices: 23.5 us -> 27.7 us
  other arithmetic: 13.5 us -> 11.2 us
    ppermute x6, waiting for transfers between devices: 23.5 us -> 27.7 us  [swap(): return lax.ppermute(block, axis, route)]
    concatenate x1 -> x0, other arithmetic: 2.3 us -> none  [shards(): partner = jnp.concatenate([lo, hi], axis=0)]
    unnamed x11 -> x7, local copies, waits for them, and re-layouts: 5.65 us -> 5.99 us
  transfers between devices with their start and end apart: 15 -> 15, of which waited for: 4 -> 5; matrix products, arithmetic and copies ran while one was open for 12% -> 11% of each run, Pallas kernels for 25% -> 24%
where the time goes in v1:
time: 115 us; the launch traced here: 114 us
  Pallas kernels  51.2 us (45%)
  waiting for transfers between devices  27.7 us (24%)
  starting transfers between devices  17.5 us (15%)
  other arithmetic  11.2 us (10%)
  local copies, waits for them, and re-layouts  6.71 us (6%)
    pallas_call x4, Pallas kernels, local_part(): pl.pallas_call(functools.partial(local_kernel, scale, rows, group), grid=...  28 us
    ppermute x6, waiting for transfers between devices, swap(): return lax.ppermute(block, axis, route)  27.7 us
    pallas_call x1, Pallas kernels, cross_all(): pl.pallas_call(functools.partial(cross_kernel, scale, rows, first_level,...  18 us
    ppermute x6, starting transfers between devices, swap(): return lax.ppermute(block, axis, route)  12.5 us
    another operation x3, other arithmetic, shards(): ctx_stacks.append(jnp.stack([parts[o] for o in range(seq_count)]))  6.67 us
    unnamed x7, local copies, waits for them, and re-layouts  5.99 us
    pallas_call x1, Pallas kernels, own_state(): pl.pallas_call(functools.partial(state_kernel, head_count), grid=(rows //...  5.25 us
    ppermute x9, starting transfers between devices, to_offset(): return lax.ppermute(block, axis, [(s, s ^ offset) for s in range(count)])  5.04 us
  transfers between devices with their start and end apart: 15, of which 5 were waited for; matrix products, arithmetic and copies ran while one was open for 11% of the time, Pallas kernels for 24%

profile of v1, /device:TPU:0, one launch (start us, length us, event | category | flops | bytes accessed | tf_op | source)
XLA Modules:
  0.0 114.4 jit_solution(18336314375797002318)
XLA Ops:
  0.0 5.3 %shard_map.59 = f32[16,128,128]{2,1,0:T(8,128)} custom-call(bf16[1024,2048]{1,0:T(8,128)(2,1)} %k_ref.9, bf16[1024,2048]{1,0:T(8,128)(2,1)} %v_ref.9), custom_call_target="tpu_custom_call" | custom-call | flops 536870912 | bytes 9437184 | tf_op jit(solution)/shard_map/pallas_call | solution.py:50
  5.3 0.5 collective-permute-start
  5.7 2.5 %collective-permute-done.rest_0_ = f32[16,128,128]{2,1,0:T(8,128)S(1)} collective-permute-done((f32[16,128,128]{2,1,0:T(8,128)}, f32[16,128,128]{2,1,0:T(8,128)S(1)}, u32[]{:S(2)}, u32[]{:S(2)}) %collective-permute-start) | collective-permute-done | bytes 1048608 | tf_op jit(solution)/shard_map/ppermute | solution.py:242
  8.2 1.7 %add.18 = f32[16,128,128]{2,1,0:T(8,128)S(1)} add(f32[16,128,128]{2,1,0:T(8,128)} %shard_map.59, f32[16,128,128]{2,1,0:T(8,128)S(1)} %collective-permute-done.rest_0_) | non-fusion elementwise | flops 262144 | bytes 3145728 | tf_op jit(solution)/shard_map/add | solution.py:286
  10.0 2.9 %collective-permute-start.1 = (f32[8,128,128]{2,1,0:T(8,128)S(1)}, f32[8,128,128]{2,1,0:T(8,128)S(1)}, u32[]{:S(2)}, u32[]{:S(2)}) collective-permute-start(f32[8,128,128]{2,1,0:T(8,128)S(1)} %constant_dynamic-slice_fusion), channel_id=1, source_target_pairs={{0,2},{2,0},{1,3},{3,1},{4,6},{6,4},{5,7},{7,5},{8,10},{10,8},{9,1... | collective-permute-start | bytes 1572872 | tf_op jit(solution)/shard_map/ppermute | solution.py:242
  12.9 12.2 %collective-permute-done.1.rest_1_ = f32[8,128,128]{2,1,0:T(8,128)S(1)} collective-permute-done((f32[8,128,128]{2,1,0:T(8,128)S(1)}, f32[8,128,128]{2,1,0:T(8,128)S(1)}, u32[]{:S(2)}, u32[]{:S(2)}) %collective-permute-start.1) | collective-permute-done | bytes 524320 | tf_op jit(solution)/shard_map/ppermute | solution.py:242
  25.2 0.0 collective-permute-start.2
  25.2 1.9 %collective-permute-done.2.rest_2_ = f32[8,128,128]{2,1,0:T(8,128)S(1)} collective-permute-done((f32[8,128,128]{2,1,0:T(8,128)S(1)}, f32[8,128,128]{2,1,0:T(8,128)S(1)}, u32[]{:S(2)}, u32[]{:S(2)}) %collective-permute-start.2) | collective-permute-done | bytes 524320 | tf_op jit(solution)/shard_map/ppermute | solution.py:242
  27.1 0.1 broadcast_select_fusion
  27.2 0.1 fusion.1
  27.2 1.8 %collective-permute-start.3 = (f32[4,128,128]{2,1,0:T(8,128)S(1)}, f32[4,128,128]{2,1,0:T(8,128)}, u32[]{:S(2)}, u32[]{:S(2)}) collective-permute-start(f32[4,128,128]{2,1,0:T(8,128)S(1)} %fusion.1), channel_id=1, source_target_pairs={{0,4},{4,0},{8,12},{12,8},{16,20},{20,16},{24,28},{28,24},{1,5},{5... | collective-permute-start | bytes 786440 | tf_op jit(solution)/shard_map/ppermute | solution.py:242
  29.1 6.7 %collective-permute-done.3 = f32[4,128,128]{2,1,0:T(8,128)} collective-permute-done((f32[4,128,128]{2,1,0:T(8,128)S(1)}, f32[4,128,128]{2,1,0:T(8,128)}, u32[]{:S(2)}, u32[]{:S(2)}) %collective-permute-start.3) | collective-permute-done | bytes 262176 | tf_op jit(solution)/shard_map/ppermute | solution.py:242
  35.8 1.0 add.22
  36.8 1.9 %collective-permute-start.7 = (f32[4,128,128]{2,1,0:T(8,128)S(1)}, f32[4,128,128]{2,1,0:T(8,128)}, u32[]{:S(2)}, u32[]{:S(2)}) collective-permute-start(f32[4,128,128]{2,1,0:T(8,128)S(1)} %add.22), channel_id=1, source_target_pairs={{0,8},{8,0},{4,12},{12,4},{16,24},{24,16},{20,28},{28,20},{1,9},{9... | collective-permute-start | bytes 786440 | tf_op jit(solution)/shard_map/ppermute | solution.py:242
  38.6 1.5 %collective-permute-start.5 = (f32[4,128,128]{2,1,0:T(8,128)}, f32[4,128,128]{2,1,0:T(8,128)}, u32[]{:S(2)}, u32[]{:S(2)}) collective-permute-start(f32[4,128,128]{2,1,0:T(8,128)} %collective-permute-done.3), channel_id=1, source_target_pairs={{0,2},{1,3},{2,0},{3,1},{4,6},{5,7},{6,4},{7,5},{8,10},{9,11},{10,... | collective-permute-start | bytes 786440 | tf_op jit(solution)/shard_map/ppermute | solution.py:247
  40.1 4.4 %collective-permute-done.7 = f32[4,128,128]{2,1,0:T(8,128)} collective-permute-done((f32[4,128,128]{2,1,0:T(8,128)S(1)}, f32[4,128,128]{2,1,0:T(8,128)}, u32[]{:S(2)}, u32[]{:S(2)}) %collective-permute-start.7) | collective-permute-done | bytes 262176 | tf_op jit(solution)/shard_map/ppermute | solution.py:242
  44.5 1.7 %add.23 = f32[4,128,128]{2,1,0:T(8,128)} add(f32[4,128,128]{2,1,0:T(8,128)S(1)} %add.22, f32[4,128,128]{2,1,0:T(8,128)} %collective-permute-done.7) | non-fusion elementwise | flops 65536 | bytes 786432 | tf_op jit(solution)/shard_map/add | solution.py:295
  46.2 5.4 %collective-permute-start.11 = (f32[4,128,128]{2,1,0:T(8,128)}, f32[4,128,128]{2,1,0:T(8,128)}, u32[]{:S(2)}, u32[]{:S(2)}) collective-permute-start(f32[4,128,128]{2,1,0:T(8,128)} %add.23), channel_id=1, source_target_pairs={{0,16},{4,20},{8,24},{12,28},{1,17},{5,21},{9,25},{13,29},{2,18},{... | collective-permute-start | bytes 786440 | tf_op jit(solution)/shard_map/ppermute | solution.py:242
  51.5 6.0 %copy.10 = f32[10,16,1024]{0,2,1:T(8,128)} copy(f32[10,16,1024]{2,1,0:T(8,128)} %param.8) | data formatting | bytes 1310720 | tf_op args[3]
  57.5 0.0 copy-done
  57.5 1.5 %collective-permute-start.9 = (f32[4,128,128]{2,1,0:T(8,128)}, f32[4,128,128]{2,1,0:T(8,128)}, u32[]{:S(2)}, u32[]{:S(2)}) collective-permute-start(f32[4,128,128]{2,1,0:T(8,128)} %collective-permute-done.7), channel_id=1, source_target_pairs={{0,2},{1,3},{2,0},{3,1},{4,6},{5,7},{6,4},{7,5},{8,10},{9,11},{10,... | collective-permute-start | bytes 786440 | tf_op jit(solution)/shard_map/ppermute | solution.py:247
  59.0 0.0 copy-done.2
  59.0 7.1 %shard_map.55.rest_0_ = f32[1024,2048]{1,0:T(8,128)} custom-call(bf16[1024,2048]{1,0:T(8,128)(2,1)} %q_ref.9, bf16[1024,2048]{1,0:T(8,128)(2,1)} %k_ref.9, bf16[1024,2048]{1,0:T(8,128)(2,1)} %v_ref.9, f32[16,1024,10]{2,1,0:T(8,128)} %bitcast.19, f32[3,256,256]{2,1,0:T(8,128)} %constant.23.clone.c_ref), custom_call_target="tpu_custom_call" | custom-call | flops 1342177280 | bytes 5242880 | tf_op jit(solution)/shard_map/pallas_call | solution.py:122
  66.1 0.0 collective-permute-start.4
  66.1 0.0 collective-permute-done.5
  66.1 0.5 collective-permute-start.6
  66.7 0.0 collective-permute-done.11
  66.7 0.5 collective-permute-start.13
  67.2 7.0 %shard_map.56.rest_0_ = f32[1024,2048]{1,0:T(8,128)} custom-call(bf16[1024,2048]{1,0:T(8,128)(2,1)} %q_ref.9, bf16[1024,2048]{1,0:T(8,128)(2,1)} %k_ref.9, bf16[1024,2048]{1,0:T(8,128)(2,1)} %v_ref.9, f32[16,1024,10]{2,1,0:T(8,128)} %bitcast.20, f32[3,256,256]{2,1,0:T(8,128)} %constant.23.clone.c_ref, ...), custom_call_target="tpu_custom_call", output_to_operand_aliasing={{}: (5, {})} | custom-call | flops 1342177280 | bytes 5242880 | tf_op jit(solution)/shard_map/pallas_call | solution.py:122
  74.2 0.7 stack.72.sp_ref
  74.8 7.0 %shard_map.57.rest_0_ = f32[1024,2048]{1,0:T(8,128)} custom-call(bf16[1024,2048]{1,0:T(8,128)(2,1)} %q_ref.9, bf16[1024,2048]{1,0:T(8,128)(2,1)} %k_ref.9, bf16[1024,2048]{1,0:T(8,128)(2,1)} %v_ref.9, f32[16,1024,10]{2,1,0:T(8,128)} %bitcast.21, f32[3,256,256]{2,1,0:T(8,128)} %constant.23.clone.c_ref, ...), custom_call_target="tpu_custom_call", output_to_operand_aliasing={{}: (5, {})} | custom-call | flops 1342177280 | bytes 5242880 | tf_op jit(solution)/shard_map/pallas_call | solution.py:122
  81.8 0.0 collective-permute-start.8
  81.8 0.0 collective-permute-done.9
  81.8 0.5 collective-permute-start.10
  82.3 7.0 %shard_map.58.l_ref = f32[1024,2048]{1,0:T(8,128)} custom-call(bf16[1024,2048]{1,0:T(8,128)(2,1)} %q_ref.9, bf16[1024,2048]{1,0:T(8,128)(2,1)} %k_ref.9, bf16[1024,2048]{1,0:T(8,128)(2,1)} %v_ref.9, f32[16,1024,10]{2,1,0:T(8,128)} %bitcast.22, f32[3,256,256]{2,1,0:T(8,128)} %constant.23.clone.c_ref, ...), custom_call_target="tpu_custom_call", output_to_operand_aliasing={{}: (5, {})} | custom-call | flops 1342177280 | bytes 5242880 | tf_op jit(solution)/shard_map/pallas_call | solution.py:122
  89.3 0.0 collective-permute-done.4
  89.3 0.1 collective-permute-start.12
  89.3 0.0 collective-permute-done.13
  89.3 0.4 collective-permute-start.14
  89.8 0.0 collective-permute-done.6
  89.8 2.3 %pad_maximum_fusion.rest_3_ = f32[4,4,128,128]{3,2,1,0:T(8,128)} fusion(f32[1,4,128,128]{3,2,1,0:T(8,128)} %bitcast.10, f32[1,4,128,128]{3,2,1,0:T(8,128)} %bitcast.9, f32[1,4,128,128]{3,2,1,0:T(8,128)} %bitcast.8, f32[1,4,128,128]{3,2,1,0:T(8,128)} %bitcast.7), kind=kLoop, calls=%fused_computation.2 | loop fusion | flops 786432 | bytes 2097152 | tf_op jit(solution)/shard_map/stack | solution.py:306
  92.1 0.0 collective-permute-done.8
  92.1 0.0 collective-permute-done.10
  92.1 2.3 %pad_maximum_fusion.1.rest_4_ = f32[4,4,128,128]{3,2,1,0:T(8,128)} fusion(f32[1,4,128,128]{3,2,1,0:T(8,128)} %bitcast.14, f32[1,4,128,128]{3,2,1,0:T(8,128)} %bitcast.13, f32[1,4,128,128]{3,2,1,0:T(8,128)} %bitcast.12, f32[1,4,128,128]{3,2,1,0:T(8,128)} %bitcast.11), kind=kLoop, calls=%fused_computation.3 | loop fusion | flops 786432 | bytes 2097152 | tf_op jit(solution)/shard_map/stack | solution.py:306
  94.3 0.0 collective-permute-done.12
  94.3 0.0 collective-permute-done.14
  94.3 2.1 %pad_maximum_fusion.2.rest_5_ = f32[4,4,128,128]{3,2,1,0:T(8,128)} fusion(f32[1,4,128,128]{3,2,1,0:T(8,128)S(1)} %bitcast.25, f32[1,4,128,128]{3,2,1,0:T(8,128)} %bitcast.17, f32[1,4,128,128]{3,2,1,0:T(8,128)S(1)} %bitcast.24, f32[1,4,128,128]{3,2,1,0:T(8,128)} %bitcast.15), kind=kLoop, calls=%fused_computation.4 | loop fusion | flops 786432 | bytes 2097152 | tf_op jit(solution)/shard_map/stack | solution.py:306
  96.5 18.0 %shard_map.60 = f32[1024,2048]{1,0:T(8,128)} custom-call(s32[6]{0:T(128)} %stack.72.sp_ref, bf16[1024,2048]{1,0:T(8,128)(2,1)} %q_ref.9, f32[16,1024,10]{2,1,0:T(8,128)} %bitcast.23, f32[1024,2048]{1,0:T(8,128)} %shard_map.58.l_ref, f32[16,128,128]{2,1,0:T(8,128)} %copy-done, f32[8,128,128]{2,1,0:T(8,128)} %copy-done.1, ...), custom_call_target="tpu_custom_call", output_to_operand_aliasing={{}: (3, {})} | custom-call | flops 2684354560 | bytes 20971520 | tf_op jit(solution)/shard_map/pallas_call | solution.py:214
  (5 shorter events, 0.1 us)
Async XLA Ops:
  5.3 3.0 %collective-permute-start = (f32[16,128,128]{2,1,0:T(8,128)}, f32[16,128,128]{2,1,0:T(8,128)S(1)}, u32[]{:S(2)}, u32[]{:S(2)}) collective-permute-start(f32[16,128,128]{2,1,0:T(8,128)} %shard_map.59), channel_id=1, source_target_pairs={{0,1},{1,0},{2,3},{3,2},{4,5},{5,4},{6,7},{7,6},{8,9},{9,8},{10,11... | collective-permute-start | bytes 3145736 | tf_op jit(solution)/shard_map/ppermute | solution.py:242
  8.2 49.3 %copy-start = (f32[16,128,128]{2,1,0:T(8,128)}, f32[16,128,128]{2,1,0:T(8,128)S(1)}, u32[]{:S(2)}) copy-start(f32[16,128,128]{2,1,0:T(8,128)S(1)} %collective-permute-done.rest_0_) | copy-start | bytes 3145732
  10.0 15.1 %collective-permute-start.1 = (f32[8,128,128]{2,1,0:T(8,128)S(1)}, f32[8,128,128]{2,1,0:T(8,128)S(1)}, u32[]{:S(2)}, u32[]{:S(2)}) collective-permute-start(f32[8,128,128]{2,1,0:T(8,128)S(1)} %constant_dynamic-slice_fusion), channel_id=1, source_target_pairs={{0,2},{2,0},{1,3},{3,1},{4,6},{6,4},{5,7},{7,5},{8,10},{10,8},{9,1... | collective-permute-start | bytes 1572872 | tf_op jit(solution)/shard_map/ppermute | solution.py:242
  25.2 33.8 %copy-start.1 = (f32[8,128,128]{2,1,0:T(8,128)}, f32[8,128,128]{2,1,0:T(8,128)S(1)}, u32[]{:S(2)}) copy-start(f32[8,128,128]{2,1,0:T(8,128)S(1)} %collective-permute-done.1.rest_1_) | copy-start | bytes 1572868
  25.2 1.9 %collective-permute-start.2 = (f32[8,128,128]{2,1,0:T(8,128)S(1)}, f32[8,128,128]{2,1,0:T(8,128)S(1)}, u32[]{:S(2)}, u32[]{:S(2)}) collective-permute-start(f32[8,128,128]{2,1,0:T(8,128)S(1)} %collective-permute-done.1.rest_1_), channel_id=1, source_target_pairs={{0,1},{1,0},{2,3},{3,2},{4,5},{5,4},{6,7},{7,6},{8,9},{9,8},{10,11... | collective-permute-start | bytes 1572872 | tf_op jit(solution)/shard_map/ppermute | solution.py:242
  27.1 31.9 %copy-start.2 = (f32[8,128,128]{2,1,0:T(8,128)}, f32[8,128,128]{2,1,0:T(8,128)S(1)}, u32[]{:S(2)}) copy-start(f32[8,128,128]{2,1,0:T(8,128)S(1)} %collective-permute-done.2.rest_2_) | copy-start | bytes 1572868
  27.2 8.5 %collective-permute-start.3 = (f32[4,128,128]{2,1,0:T(8,128)S(1)}, f32[4,128,128]{2,1,0:T(8,128)}, u32[]{:S(2)}, u32[]{:S(2)}) collective-permute-start(f32[4,128,128]{2,1,0:T(8,128)S(1)} %fusion.1), channel_id=1, source_target_pairs={{0,4},{4,0},{8,12},{12,8},{16,20},{20,16},{24,28},{28,24},{1,5},{5... | collective-permute-start | bytes 786440 | tf_op jit(solution)/shard_map/ppermute | solution.py:242
  36.8 7.7 %collective-permute-start.7 = (f32[4,128,128]{2,1,0:T(8,128)S(1)}, f32[4,128,128]{2,1,0:T(8,128)}, u32[]{:S(2)}, u32[]{:S(2)}) collective-permute-start(f32[4,128,128]{2,1,0:T(8,128)S(1)} %add.22), channel_id=1, source_target_pairs={{0,8},{8,0},{4,12},{12,4},{16,24},{24,16},{20,28},{28,20},{1,9},{9... | collective-permute-start | bytes 786440 | tf_op jit(solution)/shard_map/ppermute | solution.py:242
  38.6 27.5 %collective-permute-start.5 = (f32[4,128,128]{2,1,0:T(8,128)}, f32[4,128,128]{2,1,0:T(8,128)}, u32[]{:S(2)}, u32[]{:S(2)}) collective-permute-start(f32[4,128,128]{2,1,0:T(8,128)} %collective-permute-done.3), channel_id=1, source_target_pairs={{0,2},{1,3},{2,0},{3,1},{4,6},{5,7},{6,4},{7,5},{8,10},{9,11},{10,... | collective-permute-start | bytes 786440 | tf_op jit(solution)/shard_map/ppermute | solution.py:247
  46.2 20.5 %collective-permute-start.11 = (f32[4,128,128]{2,1,0:T(8,128)}, f32[4,128,128]{2,1,0:T(8,128)}, u32[]{:S(2)}, u32[]{:S(2)}) collective-permute-start(f32[4,128,128]{2,1,0:T(8,128)} %add.23), channel_id=1, source_target_pairs={{0,16},{4,20},{8,24},{12,28},{1,17},{5,21},{9,25},{13,29},{2,18},{... | collective-permute-start | bytes 786440 | tf_op jit(solution)/shard_map/ppermute | solution.py:242
  57.5 24.3 %collective-permute-start.9 = (f32[4,128,128]{2,1,0:T(8,128)}, f32[4,128,128]{2,1,0:T(8,128)}, u32[]{:S(2)}, u32[]{:S(2)}) collective-permute-start(f32[4,128,128]{2,1,0:T(8,128)} %collective-permute-done.7), channel_id=1, source_target_pairs={{0,2},{1,3},{2,0},{3,1},{4,6},{5,7},{6,4},{7,5},{8,10},{9,11},{10,... | collective-permute-start | bytes 786440 | tf_op jit(solution)/shard_map/ppermute | solution.py:247
  66.1 23.1 %collective-permute-start.4 = (f32[4,128,128]{2,1,0:T(8,128)}, f32[4,128,128]{2,1,0:T(8,128)}, u32[]{:S(2)}, u32[]{:S(2)}) collective-permute-start(f32[4,128,128]{2,1,0:T(8,128)} %collective-permute-done.3), channel_id=1, source_target_pairs={{0,1},{1,0},{2,3},{3,2},{4,5},{5,4},{6,7},{7,6},{8,9},{9,8},{10,11... | collective-permute-start | bytes 786440 | tf_op jit(solution)/shard_map/ppermute | solution.py:247
  66.1 23.6 %collective-permute-start.6 = (f32[4,128,128]{2,1,0:T(8,128)}, f32[4,128,128]{2,1,0:T(8,128)}, u32[]{:S(2)}, u32[]{:S(2)}) collective-permute-start(f32[4,128,128]{2,1,0:T(8,128)} %collective-permute-done.5), channel_id=1, source_target_pairs={{0,1},{1,0},{2,3},{3,2},{4,5},{5,4},{6,7},{7,6},{8,9},{9,8},{10,11... | collective-permute-start | bytes 786440 | tf_op jit(solution)/shard_map/ppermute | solution.py:247
  66.7 22.7 %collective-permute-start.13 = (f32[4,128,128]{2,1,0:T(8,128)}, f32[4,128,128]{2,1,0:T(8,128)}, u32[]{:S(2)}, u32[]{:S(2)}) collective-permute-start(f32[4,128,128]{2,1,0:T(8,128)} %collective-permute-done.11), channel_id=1, source_target_pairs={{0,2},{1,3},{2,0},{3,1},{4,6},{5,7},{6,4},{7,5},{8,10},{9,11},{10,... | collective-permute-start | bytes 786440 | tf_op jit(solution)/shard_map/ppermute | solution.py:247
  81.8 10.3 %collective-permute-start.8 = (f32[4,128,128]{2,1,0:T(8,128)}, f32[4,128,128]{2,1,0:T(8,128)}, u32[]{:S(2)}, u32[]{:S(2)}) collective-permute-start(f32[4,128,128]{2,1,0:T(8,128)} %collective-permute-done.7), channel_id=1, source_target_pairs={{0,1},{1,0},{2,3},{3,2},{4,5},{5,4},{6,7},{7,6},{8,9},{9,8},{10,11... | collective-permute-start | bytes 786440 | tf_op jit(solution)/shard_map/ppermute | solution.py:247
  81.8 10.3 %collective-permute-start.10 = (f32[4,128,128]{2,1,0:T(8,128)}, f32[4,128,128]{2,1,0:T(8,128)}, u32[]{:S(2)}, u32[]{:S(2)}) collective-permute-start(f32[4,128,128]{2,1,0:T(8,128)} %collective-permute-done.9), channel_id=1, source_target_pairs={{0,1},{1,0},{2,3},{3,2},{4,5},{5,4},{6,7},{7,6},{8,9},{9,8},{10,11... | collective-permute-start | bytes 786440 | tf_op jit(solution)/shard_map/ppermute | solution.py:247
  89.3 5.1 %collective-permute-start.12 = (f32[4,128,128]{2,1,0:T(8,128)}, f32[4,128,128]{2,1,0:T(8,128)S(1)}, u32[]{:S(2)}, u32[]{:S(2)}) collective-permute-start(f32[4,128,128]{2,1,0:T(8,128)} %collective-permute-done.11), channel_id=1, source_target_pairs={{0,1},{1,0},{2,3},{3,2},{4,5},{5,4},{6,7},{7,6},{8,9},{9,8},{10,11... | collective-permute-start | bytes 786440 | tf_op jit(solution)/shard_map/ppermute | solution.py:247
  89.3 5.0 %collective-permute-start.14 = (f32[4,128,128]{2,1,0:T(8,128)}, f32[4,128,128]{2,1,0:T(8,128)S(1)}, u32[]{:S(2)}, u32[]{:S(2)}) collective-permute-start(f32[4,128,128]{2,1,0:T(8,128)} %collective-permute-done.13), channel_id=1, source_target_pairs={{0,1},{1,0},{2,3},{3,2},{4,5},{5,4},{6,7},{7,6},{8,9},{9,8},{10,11... | collective-permute-start | bytes 786440 | tf_op jit(solution)/shard_map/ppermute | solution.py:247

commit v2 on v0

--- a/solution.py
+++ b/solution.py
@@ -250,7 +250,12 @@
             partner = swap(running, "seq", bit)
         else:
             mine = seq_place & 1
-            sent = lax.dynamic_slice_in_dim(running, mine * half, half, 0)
+            if bit == 1:
+                sent = lax.dynamic_slice_in_dim(
+                    lax.optimization_barrier(state), mine * half, half, 0
+                ) + lax.dynamic_slice_in_dim(sibs[0], mine * half, half, 0)
+            else:
+                sent = lax.dynamic_slice_in_dim(running, mine * half, half, 0)
             got = swap(sent, "seq", bit)
             other = swap(got, "seq", 0)
             lo = jnp.where(mine == 0, got, other)

time: 112 us -> 113 us (level)
    add x0 -> x1, other arithmetic: none -> 1.45 us  [shards(): lax.dynamic_slice_in_dim(lax.optimization_barrier(state), mine * half, ha...]
    unnamed x11 -> x9, local copies, waits for them, and re-layouts: 5.65 us -> 6.76 us
  transfers between devices with their start and end apart: 15 -> 15, of which waited for: 4 -> 4; matrix products, arithmetic and copies ran while one was open for 12% -> 13% of each run, Pallas kernels for 25% -> 25%
where the time goes in v2:
time: 113 us; the launch traced here: 112 us
  Pallas kernels  51 us (45%)
  waiting for transfers between devices  23.4 us (21%)
  starting transfers between devices  17.3 us (15%)
  other arithmetic  13.2 us (12%)
  local copies, waits for them, and re-layouts  7.42 us (7%)
    pallas_call x4, Pallas kernels, local_part(): pl.pallas_call(functools.partial(local_kernel, scale, rows, group), grid=...  28 us
    ppermute x6, waiting for transfers between devices, swap(): return lax.ppermute(block, axis, route)  23.3 us
    pallas_call x1, Pallas kernels, cross_all(): pl.pallas_call(functools.partial(cross_kernel, scale, rows, first_level,...  17.7 us
    ppermute x6, starting transfers between devices, swap(): return lax.ppermute(block, axis, route)  12.3 us
    unnamed x9, local copies, waits for them, and re-layouts  6.76 us
    another operation x3, other arithmetic, shards(): ctx_stacks.append(jnp.stack([parts[o] for o in range(seq_count)]))  6.53 us
    pallas_call x1, Pallas kernels, own_state(): pl.pallas_call(functools.partial(state_kernel, head_count), grid=(rows //...  5.25 us
    ppermute x9, starting transfers between devices, to_offset(): return lax.ppermute(block, axis, [(s, s ^ offset) for s in range(count)])  5.04 us
  transfers between devices with their start and end apart: 15, of which 4 were waited for; matrix products, arithmetic and copies ran while one was open for 13% of the time, Pallas kernels for 25%

profile of v2, /device:TPU:0, one launch (start us, length us, event | category | flops | bytes accessed | tf_op | source)
XLA Modules:
  0.0 112.3 jit_solution(8395668637307423998)
XLA Ops:
  0.0 5.3 %shard_map.59 = f32[16,128,128]{2,1,0:T(8,128)} custom-call(bf16[1024,2048]{1,0:T(8,128)(2,1)} %k_ref.9, bf16[1024,2048]{1,0:T(8,128)(2,1)} %v_ref.9), custom_call_target="tpu_custom_call" | custom-call | flops 536870912 | bytes 9437184 | tf_op jit(solution)/shard_map/pallas_call | solution.py:50
  5.3 0.5 collective-permute-start
  5.7 2.5 %collective-permute-done.rest_0_ = f32[16,128,128]{2,1,0:T(8,128)S(1)} collective-permute-done((f32[16,128,128]{2,1,0:T(8,128)}, f32[16,128,128]{2,1,0:T(8,128)S(1)}, u32[]{:S(2)}, u32[]{:S(2)}) %collective-permute-start) | collective-permute-done | bytes 1048608 | tf_op jit(solution)/shard_map/ppermute | solution.py:218
  8.2 1.5 %dynamic-slice_add_fusion = f32[8,128,128]{2,1,0:T(8,128)S(1)} fusion(f32[16,128,128]{2,1,0:T(8,128)S(1)} %collective-permute-done.rest_0_, s32[]{:T(128)S(6)} %select_n.20, f32[16,128,128]{2,1,0:T(8,128)} %shard_map.59), kind=kLoop, calls=%fused_computation.6 | loop fusion | flops 131072 | bytes 1572868 | tf_op jit(solution)/shard_map/add | solution.py:254
  9.7 2.9 %collective-permute-start.1 = (f32[8,128,128]{2,1,0:T(8,128)S(1)}, f32[8,128,128]{2,1,0:T(8,128)S(1)}, u32[]{:S(2)}, u32[]{:S(2)}) collective-permute-start(f32[8,128,128]{2,1,0:T(8,128)S(1)} %dynamic-slice_add_fusion), channel_id=1, source_target_pairs={{0,2},{2,0},{1,3},{3,1},{4,6},{6,4},{5,7},{7,5},{8,10},{10,8},{9,1... | collective-permute-start | bytes 1572872 | tf_op jit(solution)/shard_map/ppermute | solution.py:218
  12.6 12.2 %collective-permute-done.1 = f32[8,128,128]{2,1,0:T(8,128)S(1)} collective-permute-done((f32[8,128,128]{2,1,0:T(8,128)S(1)}, f32[8,128,128]{2,1,0:T(8,128)S(1)}, u32[]{:S(2)}, u32[]{:S(2)}) %collective-permute-start.1) | collective-permute-done | bytes 524320 | tf_op jit(solution)/shard_map/ppermute | solution.py:218
  24.8 0.0 collective-permute-start.2
  24.8 1.9 %collective-permute-done.2 = f32[8,128,128]{2,1,0:T(8,128)S(1)} collective-permute-done((f32[8,128,128]{2,1,0:T(8,128)S(1)}, f32[8,128,128]{2,1,0:T(8,128)S(1)}, u32[]{:S(2)}, u32[]{:S(2)}) %collective-permute-start.2) | collective-permute-done | bytes 524320 | tf_op jit(solution)/shard_map/ppermute | solution.py:218
  26.8 0.1 broadcast_select_fusion.1
  26.9 0.8 copy-done
  27.6 1.0 fusion.1
  28.6 1.8 %collective-permute-start.3 = (f32[4,128,128]{2,1,0:T(8,128)S(1)}, f32[4,128,128]{2,1,0:T(8,128)}, u32[]{:S(2)}, u32[]{:S(2)}) collective-permute-start(f32[4,128,128]{2,1,0:T(8,128)S(1)} %fusion.1), channel_id=1, source_target_pairs={{0,4},{4,0},{8,12},{12,8},{16,20},{20,16},{24,28},{28,24},{1,5},{5... | collective-permute-start | bytes 786440 | tf_op jit(solution)/shard_map/ppermute | solution.py:218
  30.5 6.7 %collective-permute-done.3 = f32[4,128,128]{2,1,0:T(8,128)} collective-permute-done((f32[4,128,128]{2,1,0:T(8,128)S(1)}, f32[4,128,128]{2,1,0:T(8,128)}, u32[]{:S(2)}, u32[]{:S(2)}) %collective-permute-start.3) | collective-permute-done | bytes 262176 | tf_op jit(solution)/shard_map/ppermute | solution.py:218
  37.2 1.0 add.27
  38.2 1.9 %collective-permute-start.7 = (f32[4,128,128]{2,1,0:T(8,128)S(1)}, f32[4,128,128]{2,1,0:T(8,128)S(1)}, u32[]{:S(2)}, u32[]{:S(2)}) collective-permute-start(f32[4,128,128]{2,1,0:T(8,128)S(1)} %add.27), channel_id=1, source_target_pairs={{0,8},{8,0},{4,12},{12,4},{16,24},{24,16},{20,28},{28,20},{1,9},{9... | collective-permute-start | bytes 786440 | tf_op jit(solution)/shard_map/ppermute | solution.py:218
  40.0 6.0 %copy.10 = f32[10,16,1024]{0,2,1:T(8,128)} copy(f32[10,16,1024]{2,1,0:T(8,128)} %param.8) | data formatting | bytes 1310720 | tf_op args[3]
  46.0 1.5 %collective-permute-start.5 = (f32[4,128,128]{2,1,0:T(8,128)}, f32[4,128,128]{2,1,0:T(8,128)}, u32[]{:S(2)}, u32[]{:S(2)}) collective-permute-start(f32[4,128,128]{2,1,0:T(8,128)} %collective-permute-done.3), channel_id=1, source_target_pairs={{0,2},{1,3},{2,0},{3,1},{4,6},{5,7},{6,4},{7,5},{8,10},{9,11},{10,... | collective-permute-start | bytes 786440 | tf_op jit(solution)/shard_map/ppermute | solution.py:223
  47.5 0.0 collective-permute-done.7
  47.5 0.8 add.28
  48.3 0.0 copy-done.3
  48.3 5.2 %collective-permute-start.11 = (f32[4,128,128]{2,1,0:T(8,128)}, f32[4,128,128]{2,1,0:T(8,128)}, u32[]{:S(2)}, u32[]{:S(2)}) collective-permute-start(f32[4,128,128]{2,1,0:T(8,128)} %add.28), channel_id=1, source_target_pairs={{0,16},{4,20},{8,24},{12,28},{1,17},{5,21},{9,25},{13,29},{2,18},{... | collective-permute-start | bytes 786440 | tf_op jit(solution)/shard_map/ppermute | solution.py:218
  53.5 7.1 %shard_map.55.rest_0_ = f32[1024,2048]{1,0:T(8,128)} custom-call(bf16[1024,2048]{1,0:T(8,128)(2,1)} %q_ref.9, bf16[1024,2048]{1,0:T(8,128)(2,1)} %k_ref.9, bf16[1024,2048]{1,0:T(8,128)(2,1)} %v_ref.9, f32[16,1024,10]{2,1,0:T(8,128)} %bitcast.19, f32[3,256,256]{2,1,0:T(8,128)} %constant.23.clone.c_ref), custom_call_target="tpu_custom_call" | custom-call | flops 1342177280 | bytes 5242880 | tf_op jit(solution)/shard_map/pallas_call | solution.py:122
  60.6 0.5 collective-permute-start.9
  61.2 7.0 %shard_map.56.rest_0_ = f32[1024,2048]{1,0:T(8,128)} custom-call(bf16[1024,2048]{1,0:T(8,128)(2,1)} %q_ref.9, bf16[1024,2048]{1,0:T(8,128)(2,1)} %k_ref.9, bf16[1024,2048]{1,0:T(8,128)(2,1)} %v_ref.9, f32[16,1024,10]{2,1,0:T(8,128)} %bitcast.20, f32[3,256,256]{2,1,0:T(8,128)} %constant.23.clone.c_ref, ...), custom_call_target="tpu_custom_call", output_to_operand_aliasing={{}: (5, {})} | custom-call | flops 1342177280 | bytes 5242880 | tf_op jit(solution)/shard_map/pallas_call | solution.py:122
  68.1 0.7 stack.72.sp_ref
  68.8 7.0 %shard_map.57.rest_0_ = f32[1024,2048]{1,0:T(8,128)} custom-call(bf16[1024,2048]{1,0:T(8,128)(2,1)} %q_ref.9, bf16[1024,2048]{1,0:T(8,128)(2,1)} %k_ref.9, bf16[1024,2048]{1,0:T(8,128)(2,1)} %v_ref.9, f32[16,1024,10]{2,1,0:T(8,128)} %bitcast.21, f32[3,256,256]{2,1,0:T(8,128)} %constant.23.clone.c_ref, ...), custom_call_target="tpu_custom_call", output_to_operand_aliasing={{}: (5, {})} | custom-call | flops 1342177280 | bytes 5242880 | tf_op jit(solution)/shard_map/pallas_call | solution.py:122
  75.7 0.0 collective-permute-start.4
  75.8 0.0 collective-permute-done.5
  75.8 0.5 collective-permute-start.6
  76.3 0.0 collective-permute-done.11
  76.3 1.5 %collective-permute-start.13 = (f32[4,128,128]{2,1,0:T(8,128)}, f32[4,128,128]{2,1,0:T(8,128)}, u32[]{:S(2)}, u32[]{:S(2)}) collective-permute-start(f32[4,128,128]{2,1,0:T(8,128)} %collective-permute-done.11), channel_id=1, source_target_pairs={{0,2},{1,3},{2,0},{3,1},{4,6},{5,7},{6,4},{7,5},{8,10},{9,11},{10,... | collective-permute-start | bytes 786440 | tf_op jit(solution)/shard_map/ppermute | solution.py:223
  77.8 7.0 %shard_map.58.l_ref = f32[1024,2048]{1,0:T(8,128)} custom-call(bf16[1024,2048]{1,0:T(8,128)(2,1)} %q_ref.9, bf16[1024,2048]{1,0:T(8,128)(2,1)} %k_ref.9, bf16[1024,2048]{1,0:T(8,128)(2,1)} %v_ref.9, f32[16,1024,10]{2,1,0:T(8,128)} %bitcast.22, f32[3,256,256]{2,1,0:T(8,128)} %constant.23.clone.c_ref, ...), custom_call_target="tpu_custom_call", output_to_operand_aliasing={{}: (5, {})} | custom-call | flops 1342177280 | bytes 5242880 | tf_op jit(solution)/shard_map/pallas_call | solution.py:122
  84.7 0.0 collective-permute-start.8
  84.7 0.0 collective-permute-done.9
  84.7 0.5 collective-permute-start.10
  85.2 2.3 %pad_maximum_fusion.rest_1_ = f32[16,128,128]{2,1,0:T(8,128)} fusion(f32[8,128,128]{2,1,0:T(8,128)} %copy-done.1, f32[8,128,128]{2,1,0:T(8,128)} %copy-done), kind=kLoop, calls=%fused_computation.1 | loop fusion | flops 262144 | bytes 2097152 | tf_op jit(solution)/shard_map/concatenate | solution.py:263
  87.5 0.0 collective-permute-done.4
  87.5 0.1 collective-permute-start.12
  87.6 0.0 collective-permute-done.13
  87.6 0.4 collective-permute-start.14
  88.0 0.0 collective-permute-done.6
  88.0 2.3 %pad_maximum_fusion.1.rest_2_ = f32[4,4,128,128]{3,2,1,0:T(8,128)} fusion(f32[1,4,128,128]{3,2,1,0:T(8,128)} %bitcast.10, f32[1,4,128,128]{3,2,1,0:T(8,128)} %bitcast.9, f32[1,4,128,128]{3,2,1,0:T(8,128)} %bitcast.8, f32[1,4,128,128]{3,2,1,0:T(8,128)} %bitcast.7), kind=kLoop, calls=%fused_computation.3 | loop fusion | flops 786432 | bytes 2097152 | tf_op jit(solution)/shard_map/stack | solution.py:286
  90.3 0.0 collective-permute-done.8
  90.3 0.0 collective-permute-done.10
  90.3 2.1 %pad_maximum_fusion.2.rest_3_ = f32[4,4,128,128]{3,2,1,0:T(8,128)} fusion(f32[1,4,128,128]{3,2,1,0:T(8,128)S(1)} %bitcast.26, f32[1,4,128,128]{3,2,1,0:T(8,128)} %bitcast.13, f32[1,4,128,128]{3,2,1,0:T(8,128)S(1)} %bitcast.25, f32[1,4,128,128]{3,2,1,0:T(8,128)} %bitcast.24), kind=kLoop, calls=%fused_computation.4 | loop fusion | flops 786432 | bytes 2097152 | tf_op jit(solution)/shard_map/stack | solution.py:286
  92.4 0.0 collective-permute-done.12
  92.4 2.2 %pad_maximum_fusion.3.rest_4_ = f32[4,4,128,128]{3,2,1,0:T(8,128)} fusion(f32[1,4,128,128]{3,2,1,0:T(8,128)S(1)} %bitcast.28, f32[1,4,128,128]{3,2,1,0:T(8,128)} %bitcast.17, f32[1,4,128,128]{3,2,1,0:T(8,128)S(1)} %bitcast.27, f32[1,4,128,128]{3,2,1,0:T(8,128)} %bitcast.15), kind=kLoop, calls=%fused_computation.5 | loop fusion | flops 786432 | bytes 2097152 | tf_op jit(solution)/shard_map/stack | solution.py:286
  94.6 17.7 %shard_map.60 = f32[1024,2048]{1,0:T(8,128)} custom-call(s32[6]{0:T(128)} %stack.72.sp_ref, bf16[1024,2048]{1,0:T(8,128)(2,1)} %q_ref.9, f32[16,1024,10]{2,1,0:T(8,128)} %bitcast.23, f32[1024,2048]{1,0:T(8,128)} %shard_map.58.l_ref, f32[16,128,128]{2,1,0:T(8,128)} %copy-done.2, ...), custom_call_target="tpu_custom_call", output_to_operand_aliasing={{}: (3, {})} | custom-call | flops 2684354560 | bytes 20971520 | tf_op jit(solution)/shard_map/pallas_call | solution.py:190
  (7 shorter events, 0.0 us)
Async XLA Ops:
  5.3 3.0 %collective-permute-start = (f32[16,128,128]{2,1,0:T(8,128)}, f32[16,128,128]{2,1,0:T(8,128)S(1)}, u32[]{:S(2)}, u32[]{:S(2)}) collective-permute-start(f32[16,128,128]{2,1,0:T(8,128)} %shard_map.59), channel_id=1, source_target_pairs={{0,1},{1,0},{2,3},{3,2},{4,5},{5,4},{6,7},{7,6},{8,9},{9,8},{10,11... | collective-permute-start | bytes 3145736 | tf_op jit(solution)/shard_map/ppermute | solution.py:218
  8.2 22.2 %copy-start.2 = (f32[16,128,128]{2,1,0:T(8,128)}, f32[16,128,128]{2,1,0:T(8,128)S(1)}, u32[]{:S(2)}) copy-start(f32[16,128,128]{2,1,0:T(8,128)S(1)} %collective-permute-done.rest_0_) | copy-start | bytes 3145732
  9.7 15.1 %collective-permute-start.1 = (f32[8,128,128]{2,1,0:T(8,128)S(1)}, f32[8,128,128]{2,1,0:T(8,128)S(1)}, u32[]{:S(2)}, u32[]{:S(2)}) collective-permute-start(f32[8,128,128]{2,1,0:T(8,128)S(1)} %dynamic-slice_add_fusion), channel_id=1, source_target_pairs={{0,2},{2,0},{1,3},{3,1},{4,6},{6,4},{5,7},{7,5},{8,10},{10,8},{9,1... | collective-permute-start | bytes 1572872 | tf_op jit(solution)/shard_map/ppermute | solution.py:218
  24.8 1.9 %collective-permute-start.2 = (f32[8,128,128]{2,1,0:T(8,128)S(1)}, f32[8,128,128]{2,1,0:T(8,128)S(1)}, u32[]{:S(2)}, u32[]{:S(2)}) collective-permute-start(f32[8,128,128]{2,1,0:T(8,128)S(1)} %collective-permute-done.1), channel_id=1, source_target_pairs={{0,1},{1,0},{2,3},{3,2},{4,5},{5,4},{6,7},{7,6},{8,9},{9,8},{10,11... | collective-permute-start | bytes 1572872 | tf_op jit(solution)/shard_map/ppermute | solution.py:218
  26.8 0.8 copy-start
  26.9 1.8 %copy-start.1 = (f32[8,128,128]{2,1,0:T(8,128)}, f32[8,128,128]{2,1,0:T(8,128)S(1)}, u32[]{:S(2)}) copy-start(f32[8,128,128]{2,1,0:T(8,128)S(1)} %get-tuple-element.6) | copy-start | bytes 1572868
  28.6 8.5 %collective-permute-start.3 = (f32[4,128,128]{2,1,0:T(8,128)S(1)}, f32[4,128,128]{2,1,0:T(8,128)}, u32[]{:S(2)}, u32[]{:S(2)}) collective-permute-start(f32[4,128,128]{2,1,0:T(8,128)S(1)} %fusion.1), channel_id=1, source_target_pairs={{0,4},{4,0},{8,12},{12,8},{16,20},{20,16},{24,28},{28,24},{1,5},{5... | collective-permute-start | bytes 786440 | tf_op jit(solution)/shard_map/ppermute | solution.py:218
  38.2 9.3 %collective-permute-start.7 = (f32[4,128,128]{2,1,0:T(8,128)S(1)}, f32[4,128,128]{2,1,0:T(8,128)S(1)}, u32[]{:S(2)}, u32[]{:S(2)}) collective-permute-start(f32[4,128,128]{2,1,0:T(8,128)S(1)} %add.27), channel_id=1, source_target_pairs={{0,8},{8,0},{4,12},{12,4},{16,24},{24,16},{20,28},{28,20},{1,9},{9... | collective-permute-start | bytes 786440 | tf_op jit(solution)/shard_map/ppermute | solution.py:218
  46.0 29.7 %collective-permute-start.5 = (f32[4,128,128]{2,1,0:T(8,128)}, f32[4,128,128]{2,1,0:T(8,128)}, u32[]{:S(2)}, u32[]{:S(2)}) collective-permute-start(f32[4,128,128]{2,1,0:T(8,128)} %collective-permute-done.3), channel_id=1, source_target_pairs={{0,2},{1,3},{2,0},{3,1},{4,6},{5,7},{6,4},{7,5},{8,10},{9,11},{10,... | collective-permute-start | bytes 786440 | tf_op jit(solution)/shard_map/ppermute | solution.py:223
  47.5 0.8 copy-start.3
  48.3 27.9 %collective-permute-start.11 = (f32[4,128,128]{2,1,0:T(8,128)}, f32[4,128,128]{2,1,0:T(8,128)}, u32[]{:S(2)}, u32[]{:S(2)}) collective-permute-start(f32[4,128,128]{2,1,0:T(8,128)} %add.28), channel_id=1, source_target_pairs={{0,16},{4,20},{8,24},{12,28},{1,17},{5,21},{9,25},{13,29},{2,18},{... | collective-permute-start | bytes 786440 | tf_op jit(solution)/shard_map/ppermute | solution.py:218
  60.6 24.1 %collective-permute-start.9 = (f32[4,128,128]{2,1,0:T(8,128)}, f32[4,128,128]{2,1,0:T(8,128)}, u32[]{:S(2)}, u32[]{:S(2)}) collective-permute-start(f32[4,128,128]{2,1,0:T(8,128)} %copy-done.3), channel_id=1, source_target_pairs={{0,2},{1,3},{2,0},{3,1},{4,6},{5,7},{6,4},{7,5},{8,10},{9,11},{10,... | collective-permute-start | bytes 786440 | tf_op jit(solution)/shard_map/ppermute | solution.py:223
  75.7 11.8 %collective-permute-start.4 = (f32[4,128,128]{2,1,0:T(8,128)}, f32[4,128,128]{2,1,0:T(8,128)}, u32[]{:S(2)}, u32[]{:S(2)}) collective-permute-start(f32[4,128,128]{2,1,0:T(8,128)} %collective-permute-done.3), channel_id=1, source_target_pairs={{0,1},{1,0},{2,3},{3,2},{4,5},{5,4},{6,7},{7,6},{8,9},{9,8},{10,11... | collective-permute-start | bytes 786440 | tf_op jit(solution)/shard_map/ppermute | solution.py:223
  75.8 12.3 %collective-permute-start.6 = (f32[4,128,128]{2,1,0:T(8,128)}, f32[4,128,128]{2,1,0:T(8,128)}, u32[]{:S(2)}, u32[]{:S(2)}) collective-permute-start(f32[4,128,128]{2,1,0:T(8,128)} %collective-permute-done.5), channel_id=1, source_target_pairs={{0,1},{1,0},{2,3},{3,2},{4,5},{5,4},{6,7},{7,6},{8,9},{9,8},{10,11... | collective-permute-start | bytes 786440 | tf_op jit(solution)/shard_map/ppermute | solution.py:223
  76.3 11.3 %collective-permute-start.13 = (f32[4,128,128]{2,1,0:T(8,128)}, f32[4,128,128]{2,1,0:T(8,128)}, u32[]{:S(2)}, u32[]{:S(2)}) collective-permute-start(f32[4,128,128]{2,1,0:T(8,128)} %collective-permute-done.11), channel_id=1, source_target_pairs={{0,2},{1,3},{2,0},{3,1},{4,6},{5,7},{6,4},{7,5},{8,10},{9,11},{10,... | collective-permute-start | bytes 786440 | tf_op jit(solution)/shard_map/ppermute | solution.py:223
  84.7 5.6 %collective-permute-start.8 = (f32[4,128,128]{2,1,0:T(8,128)}, f32[4,128,128]{2,1,0:T(8,128)S(1)}, u32[]{:S(2)}, u32[]{:S(2)}) collective-permute-start(f32[4,128,128]{2,1,0:T(8,128)} %copy-done.3), channel_id=1, source_target_pairs={{0,1},{1,0},{2,3},{3,2},{4,5},{5,4},{6,7},{7,6},{8,9},{9,8},{10,11... | collective-permute-start | bytes 786440 | tf_op jit(solution)/shard_map/ppermute | solution.py:223
  84.7 5.6 %collective-permute-start.10 = (f32[4,128,128]{2,1,0:T(8,128)}, f32[4,128,128]{2,1,0:T(8,128)S(1)}, u32[]{:S(2)}, u32[]{:S(2)}) collective-permute-start(f32[4,128,128]{2,1,0:T(8,128)} %collective-permute-done.9), channel_id=1, source_target_pairs={{0,1},{1,0},{2,3},{3,2},{4,5},{5,4},{6,7},{7,6},{8,9},{9,8},{10,11... | collective-permute-start | bytes 786440 | tf_op jit(solution)/shard_map/ppermute | solution.py:223
  87.5 4.9 %collective-permute-start.12 = (f32[4,128,128]{2,1,0:T(8,128)}, f32[4,128,128]{2,1,0:T(8,128)S(1)}, u32[]{:S(2)}, u32[]{:S(2)}) collective-permute-start(f32[4,128,128]{2,1,0:T(8,128)} %collective-permute-done.11), channel_id=1, source_target_pairs={{0,1},{1,0},{2,3},{3,2},{4,5},{5,4},{6,7},{7,6},{8,9},{9,8},{10,11... | collective-permute-start | bytes 786440 | tf_op jit(solution)/shard_map/ppermute | solution.py:223
  87.6 4.8 %collective-permute-start.14 = (f32[4,128,128]{2,1,0:T(8,128)}, f32[4,128,128]{2,1,0:T(8,128)S(1)}, u32[]{:S(2)}, u32[]{:S(2)}) collective-permute-start(f32[4,128,128]{2,1,0:T(8,128)} %collective-permute-done.13), channel_id=1, source_target_pairs={{0,1},{1,0},{2,3},{3,2},{4,5},{5,4},{6,7},{7,6},{8,9},{9,8},{10,11... | collective-permute-start | bytes 786440 | tf_op jit(solution)/shard_map/ppermute | solution.py:223

commit v3 on v2

--- a/solution.py
+++ b/solution.py
@@ -266,7 +266,21 @@
         running = running + partner
 
     share = head_count // seq_count
-    quarter = lax.dynamic_slice_in_dim(running, seq_place * share, share, 0)
+    if seq_bits == 2:
+        start = seq_place * share
+        inner_at = start % half
+        from_got = (seq_place >> 1) == (seq_place & 1)
+        upper = jnp.where(
+            from_got,
+            lax.dynamic_slice_in_dim(got, inner_at, share, 0),
+            lax.dynamic_slice_in_dim(other, inner_at, share, 0),
+        )
+        quarter = (
+            lax.dynamic_slice_in_dim(lax.optimization_barrier(state), start, share, 0)
+            + lax.dynamic_slice_in_dim(sibs[0], start, share, 0)
+        ) + upper
+    else:
+        quarter = lax.dynamic_slice_in_dim(running, seq_place * share, share, 0)
     ctx_sibs = []
     for bit in range(ctx_bits):
         got = swap(quarter, "ctx", bit, one_way=(bit == ctx_bits - 1))

time: 113 us -> 121 us (1.071)
  the two profiles are of different devices: /device:TPU:0 before, /device:TPU:1 now
where the time goes in v3:
time: 121 us; the launch traced here: 120 us
  Pallas kernels  50.8 us (42%)
  waiting for transfers between devices  30.1 us (25%)
  starting transfers between devices  19.1 us (16%)
  other arithmetic  13.7 us (11%)
  local copies, waits for them, and re-layouts  6.62 us (5%)
    pallas_call x4, Pallas kernels, local_part(): pl.pallas_call(functools.partial(local_kernel, scale, rows, group), grid=...  28 us
    ppermute x6, waiting for transfers between devices, swap(): return lax.ppermute(block, axis, route)  22.4 us
    pallas_call x1, Pallas kernels, cross_all(): pl.pallas_call(functools.partial(cross_kernel, scale, rows, first_level,...  17.6 us
    ppermute x6, starting transfers between devices, swap(): return lax.ppermute(block, axis, route)  11.3 us
    ppermute x9, starting transfers between devices, to_offset(): return lax.ppermute(block, axis, [(s, s ^ offset) for s in range(count)])  7.79 us
    ppermute x9, waiting for transfers between devices, to_offset(): return lax.ppermute(block, axis, [(s, s ^ offset) for s in range(count)])  7.7 us
    another operation x3, other arithmetic, shards(): ctx_stacks.append(jnp.stack([parts[o] for o in range(seq_count)]))  6.17 us
    unnamed x9, local copies, waits for them, and re-layouts  5.99 us
  transfers between devices with their start and end apart: 15, of which 6 were waited for; matrix products, arithmetic and copies ran while one was open for 12% of the time, Pallas kernels for 23%

profile of v3, /device:TPU:1, one launch (start us, length us, event | category | flops | bytes accessed | tf_op | source)
XLA Modules:
  0.0 120.3 jit_solution(16294157560859686525)
XLA Ops:
  0.0 5.3 %shard_map.59 = f32[16,128,128]{2,1,0:T(8,128)} custom-call(bf16[1024,2048]{1,0:T(8,128)(2,1)} %k_ref.9, bf16[1024,2048]{1,0:T(8,128)(2,1)} %v_ref.9), custom_call_target="tpu_custom_call" | custom-call | flops 536870912 | bytes 9437184 | tf_op jit(solution)/shard_map/pallas_call | solution.py:50
  5.3 0.0 collective-permute-start
  5.3 2.9 %collective-permute-done.rest_0_ = f32[16,128,128]{2,1,0:T(8,128)S(1)} collective-permute-done((f32[16,128,128]{2,1,0:T(8,128)}, f32[16,128,128]{2,1,0:T(8,128)S(1)}, u32[]{:S(2)}, u32[]{:S(2)}) %collective-permute-start) | collective-permute-done | bytes 1048608 | tf_op jit(solution)/shard_map/ppermute | solution.py:218
  8.1 1.5 %dynamic-slice_add_fusion = f32[8,128,128]{2,1,0:T(8,128)S(1)} fusion(f32[16,128,128]{2,1,0:T(8,128)S(1)} %collective-permute-done.rest_0_, s32[]{:T(128)S(6)} %select_n.40, f32[16,128,128]{2,1,0:T(8,128)} %shard_map.59), kind=kLoop, calls=%fused_computation.4 | loop fusion | flops 131072 | bytes 1572868 | tf_op jit(solution)/shard_map/add | solution.py:254
  9.6 2.4 %collective-permute-start.1 = (f32[8,128,128]{2,1,0:T(8,128)S(1)}, f32[8,128,128]{2,1,0:T(8,128)S(1)}, u32[]{:S(2)}, u32[]{:S(2)}) collective-permute-start(f32[8,128,128]{2,1,0:T(8,128)S(1)} %dynamic-slice_add_fusion), channel_id=1, source_target_pairs={{0,2},{2,0},{1,3},{3,1},{4,6},{6,4},{5,7},{7,5},{8,10},{10,8},{9,1... | collective-permute-start | bytes 1572872 | tf_op jit(solution)/shard_map/ppermute | solution.py:218
  12.0 11.9 %collective-permute-done.1 = f32[8,128,128]{2,1,0:T(8,128)S(1)} collective-permute-done((f32[8,128,128]{2,1,0:T(8,128)S(1)}, f32[8,128,128]{2,1,0:T(8,128)S(1)}, u32[]{:S(2)}, u32[]{:S(2)}) %collective-permute-start.1) | collective-permute-done | bytes 524320 | tf_op jit(solution)/shard_map/ppermute | solution.py:218
  23.9 0.9 collective-permute-start.2
  24.9 1.5 %collective-permute-done.2 = f32[8,128,128]{2,1,0:T(8,128)S(1)} collective-permute-done((f32[8,128,128]{2,1,0:T(8,128)S(1)}, f32[8,128,128]{2,1,0:T(8,128)S(1)}, u32[]{:S(2)}, u32[]{:S(2)}) %collective-permute-start.2) | collective-permute-done | bytes 524320 | tf_op jit(solution)/shard_map/ppermute | solution.py:218
  26.4 1.2 select_add_fusion
  27.6 1.6 %collective-permute-start.3 = (f32[4,128,128]{2,1,0:T(8,128)S(1)}, f32[4,128,128]{2,1,0:T(8,128)S(1)}, u32[]{:S(2)}, u32[]{:S(2)}) collective-permute-start(f32[4,128,128]{2,1,0:T(8,128)S(1)} %select_add_fusion), channel_id=1, source_target_pairs={{0,4},{4,0},{8,12},{12,8},{16,20},{20,16},{24,28},{28,24},{1,5},{5... | collective-permute-start | bytes 786440 | tf_op jit(solution)/shard_map/ppermute | solution.py:218
  29.1 6.1 %collective-permute-done.3 = f32[4,128,128]{2,1,0:T(8,128)S(1)} collective-permute-done((f32[4,128,128]{2,1,0:T(8,128)S(1)}, f32[4,128,128]{2,1,0:T(8,128)S(1)}, u32[]{:S(2)}, u32[]{:S(2)}) %collective-permute-start.3) | collective-permute-done | bytes 262176 | tf_op jit(solution)/shard_map/ppermute | solution.py:218
  35.2 0.8 add.38
  36.0 0.0 copy-done.3
  36.0 1.5 %collective-permute-start.7 = (f32[4,128,128]{2,1,0:T(8,128)}, f32[4,128,128]{2,1,0:T(8,128)}, u32[]{:S(2)}, u32[]{:S(2)}) collective-permute-start(f32[4,128,128]{2,1,0:T(8,128)} %add.38), channel_id=1, source_target_pairs={{0,8},{8,0},{4,12},{12,4},{16,24},{24,16},{20,28},{28,20},{1,9},{9... | collective-permute-start | bytes 786440 | tf_op jit(solution)/shard_map/ppermute | solution.py:218
  37.5 6.0 %copy.10 = f32[10,16,1024]{0,2,1:T(8,128)} copy(f32[10,16,1024]{2,1,0:T(8,128)} %param.8) | data formatting | bytes 1310720 | tf_op args[3]
  43.5 7.1 %shard_map.55.rest_0_ = f32[1024,2048]{1,0:T(8,128)} custom-call(bf16[1024,2048]{1,0:T(8,128)(2,1)} %q_ref.9, bf16[1024,2048]{1,0:T(8,128)(2,1)} %k_ref.9, bf16[1024,2048]{1,0:T(8,128)(2,1)} %v_ref.9, f32[16,1024,10]{2,1,0:T(8,128)} %bitcast.19, f32[3,256,256]{2,1,0:T(8,128)} %constant.33.clone.c_ref), custom_call_target="tpu_custom_call" | custom-call | flops 1342177280 | bytes 5242880 | tf_op jit(solution)/shard_map/pallas_call | solution.py:122
  50.6 1.2 %collective-permute-start.5 = (f32[4,128,128]{2,1,0:T(8,128)}, f32[4,128,128]{2,1,0:T(8,128)}, u32[]{:S(2)}, u32[]{:S(2)}) collective-permute-start(f32[4,128,128]{2,1,0:T(8,128)} %copy-done.3), channel_id=1, source_target_pairs={{0,2},{1,3},{2,0},{3,1},{4,6},{5,7},{6,4},{7,5},{8,10},{9,11},{10,... | collective-permute-start | bytes 786440 | tf_op jit(solution)/shard_map/ppermute | solution.py:223
  51.8 0.0 collective-permute-done.7
  51.8 1.8 %add.39 = f32[4,128,128]{2,1,0:T(8,128)} add(f32[4,128,128]{2,1,0:T(8,128)} %add.38, f32[4,128,128]{2,1,0:T(8,128)} %collective-permute-done.7) | non-fusion elementwise | flops 65536 | bytes 786432 | tf_op jit(solution)/shard_map/add | solution.py:289
  53.6 4.9 %collective-permute-start.11 = (f32[4,128,128]{2,1,0:T(8,128)}, f32[4,128,128]{2,1,0:T(8,128)}, u32[]{:S(2)}, u32[]{:S(2)}) collective-permute-start(f32[4,128,128]{2,1,0:T(8,128)} %add.39), channel_id=1, source_target_pairs={{0,16},{4,20},{8,24},{12,28},{1,17},{5,21},{9,25},{13,29},{2,18},{... | collective-permute-start | bytes 786440 | tf_op jit(solution)/shard_map/ppermute | solution.py:218
  58.5 7.0 %shard_map.56.rest_0_ = f32[1024,2048]{1,0:T(8,128)} custom-call(bf16[1024,2048]{1,0:T(8,128)(2,1)} %q_ref.9, bf16[1024,2048]{1,0:T(8,128)(2,1)} %k_ref.9, bf16[1024,2048]{1,0:T(8,128)(2,1)} %v_ref.9, f32[16,1024,10]{2,1,0:T(8,128)} %bitcast.20, f32[3,256,256]{2,1,0:T(8,128)} %constant.33.clone.c_ref, ...), custom_call_target="tpu_custom_call", output_to_operand_aliasing={{}: (5, {})} | custom-call | flops 1342177280 | bytes 5242880 | tf_op jit(solution)/shard_map/pallas_call | solution.py:122
  65.4 0.6 stack.72.sp_ref
  66.0 7.0 %shard_map.57.rest_0_ = f32[1024,2048]{1,0:T(8,128)} custom-call(bf16[1024,2048]{1,0:T(8,128)(2,1)} %q_ref.9, bf16[1024,2048]{1,0:T(8,128)(2,1)} %k_ref.9, bf16[1024,2048]{1,0:T(8,128)(2,1)} %v_ref.9, f32[16,1024,10]{2,1,0:T(8,128)} %bitcast.21, f32[3,256,256]{2,1,0:T(8,128)} %constant.33.clone.c_ref, ...), custom_call_target="tpu_custom_call", output_to_operand_aliasing={{}: (5, {})} | custom-call | flops 1342177280 | bytes 5242880 | tf_op jit(solution)/shard_map/pallas_call | solution.py:122
  73.0 7.0 %shard_map.58.l_ref = f32[1024,2048]{1,0:T(8,128)} custom-call(bf16[1024,2048]{1,0:T(8,128)(2,1)} %q_ref.9, bf16[1024,2048]{1,0:T(8,128)(2,1)} %k_ref.9, bf16[1024,2048]{1,0:T(8,128)(2,1)} %v_ref.9, f32[16,1024,10]{2,1,0:T(8,128)} %bitcast.22, f32[3,256,256]{2,1,0:T(8,128)} %constant.33.clone.c_ref, ...), custom_call_target="tpu_custom_call", output_to_operand_aliasing={{}: (5, {})} | custom-call | flops 1342177280 | bytes 5242880 | tf_op jit(solution)/shard_map/pallas_call | solution.py:122
  80.0 2.1 %collective-permute-start.4 = (f32[4,128,128]{2,1,0:T(8,128)}, f32[4,128,128]{2,1,0:T(8,128)S(1)}, u32[]{:S(2)}, u32[]{:S(2)}) collective-permute-start(f32[4,128,128]{2,1,0:T(8,128)} %copy-done.3), channel_id=1, source_target_pairs={{0,1},{1,0},{2,3},{3,2},{4,5},{5,4},{6,7},{7,6},{8,9},{9,8},{10,11... | collective-permute-start | bytes 786440 | tf_op jit(solution)/shard_map/ppermute | solution.py:223
  82.0 0.3 collective-permute-start.9
  82.3 0.0 collective-permute-done.5
  82.3 0.3 collective-permute-start.6
  82.6 0.0 collective-permute-done.11
  82.6 1.2 %collective-permute-start.13 = (f32[4,128,128]{2,1,0:T(8,128)}, f32[4,128,128]{2,1,0:T(8,128)S(1)}, u32[]{:S(2)}, u32[]{:S(2)}) collective-permute-start(f32[4,128,128]{2,1,0:T(8,128)} %collective-permute-done.11), channel_id=1, source_target_pairs={{0,2},{1,3},{2,0},{3,1},{4,6},{5,7},{6,4},{7,5},{8,10},{9,11},{10,... | collective-permute-start | bytes 786440 | tf_op jit(solution)/shard_map/ppermute | solution.py:223
  83.8 1.3 %broadcast_select_fusion.1 = (f32[8,128,128]{2,1,0:T(8,128)S(1)}, f32[8,128,128]{2,1,0:T(8,128)S(1)}) fusion(f32[8,128,128]{2,1,0:T(8,128)} %copy-done.1, f32[8,128,128]{2,1,0:T(8,128)} %copy-done.2, pred[]{:T(512)S(6)} %eq.9), kind=kLoop, calls=%fused_computation.7 | loop fusion | flops 262144 | bytes 2097153 | tf_op jit(solution)/shard_map/jit(_where)/select_n | solution.py:261
  85.1 0.6 collective-permute-start.8
  85.7 4.5 %collective-permute-done.9 = f32[4,128,128]{2,1,0:T(8,128)S(1)} collective-permute-done((f32[4,128,128]{2,1,0:T(8,128)}, f32[4,128,128]{2,1,0:T(8,128)S(1)}, u32[]{:S(2)}, u32[]{:S(2)}) %collective-permute-start.9) | collective-permute-done | bytes 262176 | tf_op jit(solution)/shard_map/ppermute | solution.py:223
  90.1 1.3 %collective-permute-start.10 = (f32[4,128,128]{2,1,0:T(8,128)S(1)}, f32[4,128,128]{2,1,0:T(8,128)S(1)}, u32[]{:S(2)}, u32[]{:S(2)}) collective-permute-start(f32[4,128,128]{2,1,0:T(8,128)S(1)} %collective-permute-done.9), channel_id=1, source_target_pairs={{0,1},{1,0},{2,3},{3,2},{4,5},{5,4},{6,7},{7,6},{8,9},{9,8},{10,11... | collective-permute-start | bytes 786440 | tf_op jit(solution)/shard_map/ppermute | solution.py:223
  91.4 1.1 pad_maximum_fusion.rest_1_
  92.5 0.0 collective-permute-done.4
  92.5 0.0 collective-permute-start.12
  92.5 3.2 %collective-permute-done.13 = f32[4,128,128]{2,1,0:T(8,128)S(1)} collective-permute-done((f32[4,128,128]{2,1,0:T(8,128)}, f32[4,128,128]{2,1,0:T(8,128)S(1)}, u32[]{:S(2)}, u32[]{:S(2)}) %collective-permute-start.13) | collective-permute-done | bytes 262176 | tf_op jit(solution)/shard_map/ppermute | solution.py:223
  95.7 0.9 collective-permute-start.14
  96.6 0.0 collective-permute-done.6
  96.6 2.1 %pad_maximum_fusion.1.rest_2_ = f32[4,4,128,128]{3,2,1,0:T(8,128)} fusion(f32[1,4,128,128]{3,2,1,0:T(8,128)S(1)} %bitcast.28, f32[1,4,128,128]{3,2,1,0:T(8,128)} %bitcast.9, f32[1,4,128,128]{3,2,1,0:T(8,128)S(1)} %bitcast.27, f32[1,4,128,128]{3,2,1,0:T(8,128)} %bitcast.24), kind=kLoop, calls=%fused_computation.1 | loop fusion | flops 786432 | bytes 2097152 | tf_op jit(solution)/shard_map/stack | solution.py:300
  98.7 0.0 collective-permute-done.8
  98.7 0.0 collective-permute-done.10
  98.7 2.0 %pad_maximum_fusion.2.rest_3_ = f32[4,4,128,128]{3,2,1,0:T(8,128)} fusion(f32[1,4,128,128]{3,2,1,0:T(8,128)S(1)} %bitcast.30, f32[1,4,128,128]{3,2,1,0:T(8,128)S(1)} %bitcast.25, f32[1,4,128,128]{3,2,1,0:T(8,128)S(1)} %bitcast.29, f32[1,4,128,128]{3,2,1,0:T(8,128)} %bitcast.11), kind=kLoop, calls=%fused_computation.2 | loop fusion | flops 786432 | bytes 2097152 | tf_op jit(solution)/shard_map/stack | solution.py:300
  100.7 0.0 collective-permute-done.12
  100.7 0.0 collective-permute-done.14
  100.7 2.1 %pad_maximum_fusion.3.rest_4_ = f32[4,4,128,128]{3,2,1,0:T(8,128)} fusion(f32[1,4,128,128]{3,2,1,0:T(8,128)S(1)} %bitcast.32, f32[1,4,128,128]{3,2,1,0:T(8,128)S(1)} %bitcast.26, f32[1,4,128,128]{3,2,1,0:T(8,128)S(1)} %bitcast.31, f32[1,4,128,128]{3,2,1,0:T(8,128)} %bitcast.15), kind=kLoop, calls=%fused_computation.3 | loop fusion | flops 786432 | bytes 2097152 | tf_op jit(solution)/shard_map/stack | solution.py:300
  102.8 17.6 %shard_map.60 = f32[1024,2048]{1,0:T(8,128)} custom-call(s32[6]{0:T(128)} %stack.72.sp_ref, bf16[1024,2048]{1,0:T(8,128)(2,1)} %q_ref.9, f32[16,1024,10]{2,1,0:T(8,128)} %bitcast.23, f32[1024,2048]{1,0:T(8,128)} %shard_map.58.l_ref, f32[16,128,128]{2,1,0:T(8,128)} %copy-done, ...), custom_call_target="tpu_custom_call", output_to_operand_aliasing={{}: (3, {})} | custom-call | flops 2684354560 | bytes 20971520 | tf_op jit(solution)/shard_map/pallas_call | solution.py:190
  (7 shorter events, 0.0 us)
Async XLA Ops:
  5.3 2.9 %collective-permute-start = (f32[16,128,128]{2,1,0:T(8,128)}, f32[16,128,128]{2,1,0:T(8,128)S(1)}, u32[]{:S(2)}, u32[]{:S(2)}) collective-permute-start(f32[16,128,128]{2,1,0:T(8,128)} %shard_map.59), channel_id=1, source_target_pairs={{0,1},{1,0},{2,3},{3,2},{4,5},{5,4},{6,7},{7,6},{8,9},{9,8},{10,11... | collective-permute-start | bytes 3145736 | tf_op jit(solution)/shard_map/ppermute | solution.py:218
  8.1 18.3 %copy-start = (f32[16,128,128]{2,1,0:T(8,128)}, f32[16,128,128]{2,1,0:T(8,128)S(1)}, u32[]{:S(2)}) copy-start(f32[16,128,128]{2,1,0:T(8,128)S(1)} %collective-permute-done.rest_0_) | copy-start | bytes 3145732
  9.6 14.3 %collective-permute-start.1 = (f32[8,128,128]{2,1,0:T(8,128)S(1)}, f32[8,128,128]{2,1,0:T(8,128)S(1)}, u32[]{:S(2)}, u32[]{:S(2)}) collective-permute-start(f32[8,128,128]{2,1,0:T(8,128)S(1)} %dynamic-slice_add_fusion), channel_id=1, source_target_pairs={{0,2},{2,0},{1,3},{3,1},{4,6},{6,4},{5,7},{7,5},{8,10},{10,8},{9,1... | collective-permute-start | bytes 1572872 | tf_op jit(solution)/shard_map/ppermute | solution.py:218
  23.9 3.7 %copy-start.1 = (f32[8,128,128]{2,1,0:T(8,128)}, f32[8,128,128]{2,1,0:T(8,128)S(1)}, u32[]{:S(2)}) copy-start(f32[8,128,128]{2,1,0:T(8,128)S(1)} %collective-permute-done.1) | copy-start | bytes 1572868
  23.9 2.5 %collective-permute-start.2 = (f32[8,128,128]{2,1,0:T(8,128)S(1)}, f32[8,128,128]{2,1,0:T(8,128)S(1)}, u32[]{:S(2)}, u32[]{:S(2)}) collective-permute-start(f32[8,128,128]{2,1,0:T(8,128)S(1)} %collective-permute-done.1), channel_id=1, source_target_pairs={{0,1},{1,0},{2,3},{3,2},{4,5},{5,4},{6,7},{7,6},{8,9},{9,8},{10,11... | collective-permute-start | bytes 1572872 | tf_op jit(solution)/shard_map/ppermute | solution.py:218
  26.4 2.7 %copy-start.2 = (f32[8,128,128]{2,1,0:T(8,128)}, f32[8,128,128]{2,1,0:T(8,128)S(1)}, u32[]{:S(2)}) copy-start(f32[8,128,128]{2,1,0:T(8,128)S(1)} %collective-permute-done.2) | copy-start | bytes 1572868
  27.6 7.6 %collective-permute-start.3 = (f32[4,128,128]{2,1,0:T(8,128)S(1)}, f32[4,128,128]{2,1,0:T(8,128)S(1)}, u32[]{:S(2)}, u32[]{:S(2)}) collective-permute-start(f32[4,128,128]{2,1,0:T(8,128)S(1)} %select_add_fusion), channel_id=1, source_target_pairs={{0,4},{4,0},{8,12},{12,8},{16,20},{20,16},{24,28},{28,24},{1,5},{5... | collective-permute-start | bytes 786440 | tf_op jit(solution)/shard_map/ppermute | solution.py:218
  35.2 0.8 copy-start.3
  36.0 15.8 %collective-permute-start.7 = (f32[4,128,128]{2,1,0:T(8,128)}, f32[4,128,128]{2,1,0:T(8,128)}, u32[]{:S(2)}, u32[]{:S(2)}) collective-permute-start(f32[4,128,128]{2,1,0:T(8,128)} %add.38), channel_id=1, source_target_pairs={{0,8},{8,0},{4,12},{12,4},{16,24},{24,16},{20,28},{28,20},{1,9},{9... | collective-permute-start | bytes 786440 | tf_op jit(solution)/shard_map/ppermute | solution.py:218
  50.6 31.7 %collective-permute-start.5 = (f32[4,128,128]{2,1,0:T(8,128)}, f32[4,128,128]{2,1,0:T(8,128)}, u32[]{:S(2)}, u32[]{:S(2)}) collective-permute-start(f32[4,128,128]{2,1,0:T(8,128)} %copy-done.3), channel_id=1, source_target_pairs={{0,2},{1,3},{2,0},{3,1},{4,6},{5,7},{6,4},{7,5},{8,10},{9,11},{10,... | collective-permute-start | bytes 786440 | tf_op jit(solution)/shard_map/ppermute | solution.py:223
  53.6 29.0 %collective-permute-start.11 = (f32[4,128,128]{2,1,0:T(8,128)}, f32[4,128,128]{2,1,0:T(8,128)}, u32[]{:S(2)}, u32[]{:S(2)}) collective-permute-start(f32[4,128,128]{2,1,0:T(8,128)} %add.39), channel_id=1, source_target_pairs={{0,16},{4,20},{8,24},{12,28},{1,17},{5,21},{9,25},{13,29},{2,18},{... | collective-permute-start | bytes 786440 | tf_op jit(solution)/shard_map/ppermute | solution.py:218
  80.0 12.5 %collective-permute-start.4 = (f32[4,128,128]{2,1,0:T(8,128)}, f32[4,128,128]{2,1,0:T(8,128)S(1)}, u32[]{:S(2)}, u32[]{:S(2)}) collective-permute-start(f32[4,128,128]{2,1,0:T(8,128)} %copy-done.3), channel_id=1, source_target_pairs={{0,1},{1,0},{2,3},{3,2},{4,5},{5,4},{6,7},{7,6},{8,9},{9,8},{10,11... | collective-permute-start | bytes 786440 | tf_op jit(solution)/shard_map/ppermute | solution.py:223
  82.0 8.1 %collective-permute-start.9 = (f32[4,128,128]{2,1,0:T(8,128)}, f32[4,128,128]{2,1,0:T(8,128)S(1)}, u32[]{:S(2)}, u32[]{:S(2)}) collective-permute-start(f32[4,128,128]{2,1,0:T(8,128)} %collective-permute-done.7), channel_id=1, source_target_pairs={{0,2},{1,3},{2,0},{3,1},{4,6},{5,7},{6,4},{7,5},{8,10},{9,11},{10,... | collective-permute-start | bytes 786440 | tf_op jit(solution)/shard_map/ppermute | solution.py:223
  82.3 14.3 %collective-permute-start.6 = (f32[4,128,128]{2,1,0:T(8,128)}, f32[4,128,128]{2,1,0:T(8,128)S(1)}, u32[]{:S(2)}, u32[]{:S(2)}) collective-permute-start(f32[4,128,128]{2,1,0:T(8,128)} %collective-permute-done.5), channel_id=1, source_target_pairs={{0,1},{1,0},{2,3},{3,2},{4,5},{5,4},{6,7},{7,6},{8,9},{9,8},{10,11... | collective-permute-start | bytes 786440 | tf_op jit(solution)/shard_map/ppermute | solution.py:223
  82.6 13.1 %collective-permute-start.13 = (f32[4,128,128]{2,1,0:T(8,128)}, f32[4,128,128]{2,1,0:T(8,128)S(1)}, u32[]{:S(2)}, u32[]{:S(2)}) collective-permute-start(f32[4,128,128]{2,1,0:T(8,128)} %collective-permute-done.11), channel_id=1, source_target_pairs={{0,2},{1,3},{2,0},{3,1},{4,6},{5,7},{6,4},{7,5},{8,10},{9,11},{10,... | collective-permute-start | bytes 786440 | tf_op jit(solution)/shard_map/ppermute | solution.py:223
  85.1 13.6 %collective-permute-start.8 = (f32[4,128,128]{2,1,0:T(8,128)}, f32[4,128,128]{2,1,0:T(8,128)S(1)}, u32[]{:S(2)}, u32[]{:S(2)}) collective-permute-start(f32[4,128,128]{2,1,0:T(8,128)} %collective-permute-done.7), channel_id=1, source_target_pairs={{0,1},{1,0},{2,3},{3,2},{4,5},{5,4},{6,7},{7,6},{8,9},{9,8},{10,11... | collective-permute-start | bytes 786440 | tf_op jit(solution)/shard_map/ppermute | solution.py:223
  90.1 8.6 %collective-permute-start.10 = (f32[4,128,128]{2,1,0:T(8,128)S(1)}, f32[4,128,128]{2,1,0:T(8,128)S(1)}, u32[]{:S(2)}, u32[]{:S(2)}) collective-permute-start(f32[4,128,128]{2,1,0:T(8,128)S(1)} %collective-permute-done.9), channel_id=1, source_target_pairs={{0,1},{1,0},{2,3},{3,2},{4,5},{5,4},{6,7},{7,6},{8,9},{9,8},{10,11... | collective-permute-start | bytes 786440 | tf_op jit(solution)/shard_map/ppermute | solution.py:223
  92.5 8.2 %collective-permute-start.12 = (f32[4,128,128]{2,1,0:T(8,128)}, f32[4,128,128]{2,1,0:T(8,128)S(1)}, u32[]{:S(2)}, u32[]{:S(2)}) collective-permute-start(f32[4,128,128]{2,1,0:T(8,128)} %collective-permute-done.11), channel_id=1, source_target_pairs={{0,1},{1,0},{2,3},{3,2},{4,5},{5,4},{6,7},{7,6},{8,9},{9,8},{10,11... | collective-permute-start | bytes 786440 | tf_op jit(solution)/shard_map/ppermute | solution.py:223
  95.7 5.0 %collective-permute-start.14 = (f32[4,128,128]{2,1,0:T(8,128)S(1)}, f32[4,128,128]{2,1,0:T(8,128)S(1)}, u32[]{:S(2)}, u32[]{:S(2)}) collective-permute-start(f32[4,128,128]{2,1,0:T(8,128)S(1)} %collective-permute-done.13), channel_id=1, source_target_pairs={{0,1},{1,0},{2,3},{3,2},{4,5},{5,4},{6,7},{7,6},{8,9},{9,8},{10,11... | collective-permute-start | bytes 786440 | tf_op jit(solution)/shard_map/ppermute | solution.py:223

commit v4 on v3

--- a/solution.py
+++ b/solution.py
@@ -246,14 +246,22 @@
     running = state
     half = head_count // 2
     for bit in range(seq_bits):
-        if bit == 0 or seq_count < 4:
+        if bit == 0 and seq_count >= 4:
+            mine = seq_place & 1
+            needed = swap(lax.dynamic_slice_in_dim(state, (1 - mine) * half, half, 0), "seq", 0)
+            rest_half = swap(lax.dynamic_slice_in_dim(state, mine * half, half, 0), "seq", 0)
+            partner = jnp.concatenate(
+                [jnp.where(mine == 0, needed, rest_half), jnp.where(mine == 0, rest_half, needed)],
+                axis=0,
+            )
+        elif bit == 0 or seq_count < 4:
             partner = swap(running, "seq", bit)
         else:
             mine = seq_place & 1
             if bit == 1:
                 sent = lax.dynamic_slice_in_dim(
                     lax.optimization_barrier(state), mine * half, half, 0
-                ) + lax.dynamic_slice_in_dim(sibs[0], mine * half, half, 0)
+                ) + lax.optimization_barrier(needed)
             else:
                 sent = lax.dynamic_slice_in_dim(running, mine * half, half, 0)
             got = swap(sent, "seq", bit)

time: 121 us -> 117 us (0.967)
  waiting for transfers between devices: 30.1 us -> 22.4 us
  other arithmetic: 13.7 us -> 15.7 us
  local copies, waits for them, and re-layouts: 6.62 us -> 7.89 us
    ppermute x6 -> x7, waiting for transfers between devices: 22.4 us -> 14.7 us  [swap(): return lax.ppermute(block, axis, route)]
    concatenate x0 -> x1, other arithmetic: none -> 2.35 us  [shards(): jnp.concatenate([jnp.where(mine == 0, needed, rest_half), jnp.where(mine...]
    dynamic_slice x0 -> x1, local copies, waits for them, and re-layouts: none -> 1.27 us  [shards(): lax.dynamic_slice_in_dim(state, (1 - mine) * half, half, 0)]
    ppermute x6 -> x7, starting transfers between devices: 11.3 us -> 12 us  [swap(): return lax.ppermute(block, axis, route)]
    unnamed x9 -> x11, local copies, waits for them, and re-layouts: 5.99 us -> 6 us
  transfers between devices with their start and end apart: 15 -> 16, of which waited for: 6 -> 6; matrix products, arithmetic and copies ran while one was open for 12% -> 15% of each run, Pallas kernels for 23% -> 24%
where the time goes in v4:
time: 117 us
  Pallas kernels  50.8 us (43%)
  waiting for transfers between devices  22.4 us (19%)
  starting transfers between devices  19.8 us (17%)
  other arithmetic  15.7 us (13%)
  local copies, waits for them, and re-layouts  7.89 us (7%)
    pallas_call x4, Pallas kernels, local_part(): pl.pallas_call(functools.partial(local_kernel, scale, rows, group), grid=...  28 us
    pallas_call x1, Pallas kernels, cross_all(): pl.pallas_call(functools.partial(cross_kernel, scale, rows, first_level,...  17.6 us
    ppermute x7, waiting for transfers between devices, swap(): return lax.ppermute(block, axis, route)  14.7 us
    ppermute x7, starting transfers between devices, swap(): return lax.ppermute(block, axis, route)  12 us
    ppermute x9, starting transfers between devices, to_offset(): return lax.ppermute(block, axis, [(s, s ^ offset) for s in range(count)])  7.79 us
    ppermute x9, waiting for transfers between devices, to_offset(): return lax.ppermute(block, axis, [(s, s ^ offset) for s in range(count)])  7.69 us
    another operation x3, other arithmetic, shards(): ctx_stacks.append(jnp.stack([parts[o] for o in range(seq_count)]))  6.17 us
    unnamed x11, local copies, waits for them, and re-layouts  6 us
  transfers between devices with their start and end apart: 16, of which 6 were waited for; matrix products, arithmetic and copies ran while one was open for 15% of the time, Pallas kernels for 24%

profile of v4, /device:TPU:1, one launch (start us, length us, event | category | flops | bytes accessed | tf_op | source)
XLA Modules:
  0.0 116.7 jit_solution(10645769871476553199)
XLA Ops:
  0.0 5.3 %shard_map.59 = f32[16,128,128]{2,1,0:T(8,128)} custom-call(bf16[1024,2048]{1,0:T(8,128)(2,1)} %k_ref.9, bf16[1024,2048]{1,0:T(8,128)(2,1)} %v_ref.9), custom_call_target="tpu_custom_call" | custom-call | flops 536870912 | bytes 9437184 | tf_op jit(solution)/shard_map/pallas_call | solution.py:50
  5.3 1.3 %constant_dynamic-slice_fusion.1 = (f32[8,128,128]{2,1,0:T(8,128)S(1)}, f32[8,128,128]{2,1,0:T(8,128)S(1)}) fusion(f32[16,128,128]{2,1,0:T(8,128)} %shard_map.59, s32[]{:T(128)S(6)} %select_n.51, s32[]{:T(128)S(6)} %select_n.52), kind=kLoop, calls=%fused_computation.16 | loop fusion | bytes 2097160 | tf_op jit(solution)/shard_map/dynamic_slice | solution.py:251
  6.5 0.1 collective-permute-start
  6.6 1.9 %collective-permute-done = f32[8,128,128]{2,1,0:T(8,128)S(1)} collective-permute-done((f32[8,128,128]{2,1,0:T(8,128)S(1)}, f32[8,128,128]{2,1,0:T(8,128)S(1)}, u32[]{:S(2)}, u32[]{:S(2)}) %collective-permute-start) | collective-permute-done | bytes 524320 | tf_op jit(solution)/shard_map/ppermute | solution.py:218
  8.5 1.1 dynamic-slice_add_fusion
  9.6 2.4 %collective-permute-start.2 = (f32[8,128,128]{2,1,0:T(8,128)S(1)}, f32[8,128,128]{2,1,0:T(8,128)S(1)}, u32[]{:S(2)}, u32[]{:S(2)}) collective-permute-start(f32[8,128,128]{2,1,0:T(8,128)S(1)} %dynamic-slice_add_fusion), channel_id=1, source_target_pairs={{0,2},{2,0},{1,3},{3,1},{4,6},{6,4},{5,7},{7,5},{8,10},{10,8},{9,1... | collective-permute-start | bytes 1572872 | tf_op jit(solution)/shard_map/ppermute | solution.py:218
  12.0 0.7 collective-permute-start.1
  12.7 11.3 %collective-permute-done.2 = f32[8,128,128]{2,1,0:T(8,128)S(1)} collective-permute-done((f32[8,128,128]{2,1,0:T(8,128)S(1)}, f32[8,128,128]{2,1,0:T(8,128)S(1)}, u32[]{:S(2)}, u32[]{:S(2)}) %collective-permute-start.2) | collective-permute-done | bytes 524320 | tf_op jit(solution)/shard_map/ppermute | solution.py:218
  23.9 0.9 collective-permute-start.3
  24.9 0.0 collective-permute-done.1
  24.9 0.1 broadcast_select_fusion.3
  25.0 1.4 %collective-permute-done.3 = f32[8,128,128]{2,1,0:T(8,128)S(1)} collective-permute-done((f32[8,128,128]{2,1,0:T(8,128)S(1)}, f32[8,128,128]{2,1,0:T(8,128)S(1)}, u32[]{:S(2)}, u32[]{:S(2)}) %collective-permute-start.3) | collective-permute-done | bytes 524320 | tf_op jit(solution)/shard_map/ppermute | solution.py:218
  26.4 1.2 %fusion.2 = f32[4,128,128]{2,1,0:T(8,128)S(1)} fusion(s32[]{:T(128)S(6)} %select_n.57, f32[8,128,128]{2,1,0:T(8,128)S(1)} %get-tuple-element.7, f32[8,128,128]{2,1,0:T(8,128)S(1)} %get-tuple-element.8, f32[8,128,128]{2,1,0:T(8,128)S(1)} %collective-permute-done.3, s32[]{:T(128)S(6)} %select_n.60, f32[8,128,128]{2,1,0:T(8,128)S(1)} %collective-permute-done.2, ...), kind=kLoop, calls=%fused_computation.10 | loop fusion | flops 262144 | bytes 2097161 | tf_op jit(solution)/shard_map/add | solution.py:286
  27.6 1.6 %collective-permute-start.4 = (f32[4,128,128]{2,1,0:T(8,128)S(1)}, f32[4,128,128]{2,1,0:T(8,128)S(1)}, u32[]{:S(2)}, u32[]{:S(2)}) collective-permute-start(f32[4,128,128]{2,1,0:T(8,128)S(1)} %fusion.2), channel_id=1, source_target_pairs={{0,4},{4,0},{8,12},{12,8},{16,20},{20,16},{24,28},{28,24},{1,5},{5... | collective-permute-start | bytes 786440 | tf_op jit(solution)/shard_map/ppermute | solution.py:218
  29.2 6.0 %copy.10 = f32[10,16,1024]{0,2,1:T(8,128)} copy(f32[10,16,1024]{2,1,0:T(8,128)} %param.8) | data formatting | bytes 1310720 | tf_op args[3]
  35.1 0.1 collective-permute-done.4
  35.2 0.8 add.42
  36.0 0.0 copy-done.4
  36.0 1.5 %collective-permute-start.8 = (f32[4,128,128]{2,1,0:T(8,128)}, f32[4,128,128]{2,1,0:T(8,128)}, u32[]{:S(2)}, u32[]{:S(2)}) collective-permute-start(f32[4,128,128]{2,1,0:T(8,128)} %add.42), channel_id=1, source_target_pairs={{0,8},{8,0},{4,12},{12,4},{16,24},{24,16},{20,28},{28,20},{1,9},{9... | collective-permute-start | bytes 786440 | tf_op jit(solution)/shard_map/ppermute | solution.py:218
  37.5 7.1 %shard_map.55.rest_0_ = f32[1024,2048]{1,0:T(8,128)} custom-call(bf16[1024,2048]{1,0:T(8,128)(2,1)} %q_ref.9, bf16[1024,2048]{1,0:T(8,128)(2,1)} %k_ref.9, bf16[1024,2048]{1,0:T(8,128)(2,1)} %v_ref.9, f32[16,1024,10]{2,1,0:T(8,128)} %bitcast.19, f32[3,256,256]{2,1,0:T(8,128)} %constant.33.clone.c_ref), custom_call_target="tpu_custom_call" | custom-call | flops 1342177280 | bytes 5242880 | tf_op jit(solution)/shard_map/pallas_call | solution.py:122
  44.6 0.6 stack.72.sp_ref
  45.3 7.0 %shard_map.56.rest_0_ = f32[1024,2048]{1,0:T(8,128)} custom-call(bf16[1024,2048]{1,0:T(8,128)(2,1)} %q_ref.9, bf16[1024,2048]{1,0:T(8,128)(2,1)} %k_ref.9, bf16[1024,2048]{1,0:T(8,128)(2,1)} %v_ref.9, f32[16,1024,10]{2,1,0:T(8,128)} %bitcast.20, f32[3,256,256]{2,1,0:T(8,128)} %constant.33.clone.c_ref, ...), custom_call_target="tpu_custom_call", output_to_operand_aliasing={{}: (5, {})} | custom-call | flops 1342177280 | bytes 5242880 | tf_op jit(solution)/shard_map/pallas_call | solution.py:122
  52.2 7.0 %shard_map.57.rest_0_ = f32[1024,2048]{1,0:T(8,128)} custom-call(bf16[1024,2048]{1,0:T(8,128)(2,1)} %q_ref.9, bf16[1024,2048]{1,0:T(8,128)(2,1)} %k_ref.9, bf16[1024,2048]{1,0:T(8,128)(2,1)} %v_ref.9, f32[16,1024,10]{2,1,0:T(8,128)} %bitcast.21, f32[3,256,256]{2,1,0:T(8,128)} %constant.33.clone.c_ref, ...), custom_call_target="tpu_custom_call", output_to_operand_aliasing={{}: (5, {})} | custom-call | flops 1342177280 | bytes 5242880 | tf_op jit(solution)/shard_map/pallas_call | solution.py:122
  59.2 1.2 %collective-permute-start.6 = (f32[4,128,128]{2,1,0:T(8,128)}, f32[4,128,128]{2,1,0:T(8,128)}, u32[]{:S(2)}, u32[]{:S(2)}) collective-permute-start(f32[4,128,128]{2,1,0:T(8,128)} %copy-done.4), channel_id=1, source_target_pairs={{0,2},{1,3},{2,0},{3,1},{4,6},{5,7},{6,4},{7,5},{8,10},{9,11},{10,... | collective-permute-start | bytes 786440 | tf_op jit(solution)/shard_map/ppermute | solution.py:223
  60.4 0.0 collective-permute-done.8
  60.4 1.7 %add.43 = f32[4,128,128]{2,1,0:T(8,128)} add(f32[4,128,128]{2,1,0:T(8,128)} %add.42, f32[4,128,128]{2,1,0:T(8,128)} %collective-permute-done.8) | non-fusion elementwise | flops 65536 | bytes 786432 | tf_op jit(solution)/shard_map/add | solution.py:297
  62.1 4.9 %collective-permute-start.12 = (f32[4,128,128]{2,1,0:T(8,128)}, f32[4,128,128]{2,1,0:T(8,128)}, u32[]{:S(2)}, u32[]{:S(2)}) collective-permute-start(f32[4,128,128]{2,1,0:T(8,128)} %add.43), channel_id=1, source_target_pairs={{0,16},{4,20},{8,24},{12,28},{1,17},{5,21},{9,25},{13,29},{2,18},{... | collective-permute-start | bytes 786440 | tf_op jit(solution)/shard_map/ppermute | solution.py:218
  67.1 7.0 %shard_map.58.l_ref = f32[1024,2048]{1,0:T(8,128)} custom-call(bf16[1024,2048]{1,0:T(8,128)(2,1)} %q_ref.9, bf16[1024,2048]{1,0:T(8,128)(2,1)} %k_ref.9, bf16[1024,2048]{1,0:T(8,128)(2,1)} %v_ref.9, f32[16,1024,10]{2,1,0:T(8,128)} %bitcast.22, f32[3,256,256]{2,1,0:T(8,128)} %constant.33.clone.c_ref, ...), custom_call_target="tpu_custom_call", output_to_operand_aliasing={{}: (5, {})} | custom-call | flops 1342177280 | bytes 5242880 | tf_op jit(solution)/shard_map/pallas_call | solution.py:122
  74.0 2.4 %pad_maximum_fusion.rest_0_ = f32[16,128,128]{2,1,0:T(8,128)} fusion(f32[8,128,128]{2,1,0:T(8,128)} %copy-done.1, f32[8,128,128]{2,1,0:T(8,128)} %copy-done), kind=kLoop, calls=%fused_computation.1 | loop fusion | flops 262144 | bytes 2097152 | tf_op jit(solution)/shard_map/concatenate | solution.py:253
  76.4 2.1 %collective-permute-start.5 = (f32[4,128,128]{2,1,0:T(8,128)}, f32[4,128,128]{2,1,0:T(8,128)S(1)}, u32[]{:S(2)}, u32[]{:S(2)}) collective-permute-start(f32[4,128,128]{2,1,0:T(8,128)} %copy-done.4), channel_id=1, source_target_pairs={{0,1},{1,0},{2,3},{3,2},{4,5},{5,4},{6,7},{7,6},{8,9},{9,8},{10,11... | collective-permute-start | bytes 786440 | tf_op jit(solution)/shard_map/ppermute | solution.py:223
  78.4 0.3 collective-permute-start.10
  78.7 0.0 collective-permute-done.6
  78.7 0.3 collective-permute-start.7
  79.0 1.2 %collective-permute-start.14 = (f32[4,128,128]{2,1,0:T(8,128)}, f32[4,128,128]{2,1,0:T(8,128)S(1)}, u32[]{:S(2)}, u32[]{:S(2)}) collective-permute-start(f32[4,128,128]{2,1,0:T(8,128)} %collective-permute-done.12), channel_id=1, source_target_pairs={{0,2},{1,3},{2,0},{3,1},{4,6},{5,7},{6,4},{7,5},{8,10},{9,11},{10,... | collective-permute-start | bytes 786440 | tf_op jit(solution)/shard_map/ppermute | solution.py:223
  80.2 1.3 %broadcast_select_fusion.1 = (f32[8,128,128]{2,1,0:T(8,128)S(1)}, f32[8,128,128]{2,1,0:T(8,128)S(1)}) fusion(f32[8,128,128]{2,1,0:T(8,128)} %copy-done.2, f32[8,128,128]{2,1,0:T(8,128)} %copy-done.3, pred[]{:T(512)S(6)} %eq.6), kind=kLoop, calls=%fused_computation.12 | loop fusion | flops 262144 | bytes 2097153 | tf_op jit(solution)/shard_map/jit(_where)/select_n | solution.py:269
  81.5 0.6 collective-permute-start.9
  82.1 4.5 %collective-permute-done.10 = f32[4,128,128]{2,1,0:T(8,128)S(1)} collective-permute-done((f32[4,128,128]{2,1,0:T(8,128)}, f32[4,128,128]{2,1,0:T(8,128)S(1)}, u32[]{:S(2)}, u32[]{:S(2)}) %collective-permute-start.10) | collective-permute-done | bytes 262176 | tf_op jit(solution)/shard_map/ppermute | solution.py:223
  86.5 1.3 %collective-permute-start.11 = (f32[4,128,128]{2,1,0:T(8,128)S(1)}, f32[4,128,128]{2,1,0:T(8,128)S(1)}, u32[]{:S(2)}, u32[]{:S(2)}) collective-permute-start(f32[4,128,128]{2,1,0:T(8,128)S(1)} %collective-permute-done.10), channel_id=1, source_target_pairs={{0,1},{1,0},{2,3},{3,2},{4,5},{5,4},{6,7},{7,6},{8,9},{9,8},{10,11... | collective-permute-start | bytes 786440 | tf_op jit(solution)/shard_map/ppermute | solution.py:223
  87.8 1.1 pad_maximum_fusion.1.rest_1_
  88.9 0.0 collective-permute-done.5
  88.9 0.0 collective-permute-start.13
  88.9 3.2 %collective-permute-done.14 = f32[4,128,128]{2,1,0:T(8,128)S(1)} collective-permute-done((f32[4,128,128]{2,1,0:T(8,128)}, f32[4,128,128]{2,1,0:T(8,128)S(1)}, u32[]{:S(2)}, u32[]{:S(2)}) %collective-permute-start.14) | collective-permute-done | bytes 262176 | tf_op jit(solution)/shard_map/ppermute | solution.py:223
  92.1 0.9 collective-permute-start.15
  93.0 2.1 %pad_maximum_fusion.2.rest_2_ = f32[4,4,128,128]{3,2,1,0:T(8,128)} fusion(f32[1,4,128,128]{3,2,1,0:T(8,128)S(1)} %bitcast.28, f32[1,4,128,128]{3,2,1,0:T(8,128)} %bitcast.9, f32[1,4,128,128]{3,2,1,0:T(8,128)S(1)} %bitcast.27, f32[1,4,128,128]{3,2,1,0:T(8,128)} %bitcast.24), kind=kLoop, calls=%fused_computation.4 | loop fusion | flops 786432 | bytes 2097152 | tf_op jit(solution)/shard_map/stack | solution.py:308
  95.1 2.0 %pad_maximum_fusion.3.rest_3_ = f32[4,4,128,128]{3,2,1,0:T(8,128)} fusion(f32[1,4,128,128]{3,2,1,0:T(8,128)S(1)} %bitcast.30, f32[1,4,128,128]{3,2,1,0:T(8,128)S(1)} %bitcast.25, f32[1,4,128,128]{3,2,1,0:T(8,128)S(1)} %bitcast.29, f32[1,4,128,128]{3,2,1,0:T(8,128)} %bitcast.11), kind=kLoop, calls=%fused_computation.5 | loop fusion | flops 786432 | bytes 2097152 | tf_op jit(solution)/shard_map/stack | solution.py:308
  97.1 0.0 collective-permute-done.13
  97.1 2.1 %pad_maximum_fusion.4.rest_4_ = f32[4,4,128,128]{3,2,1,0:T(8,128)} fusion(f32[1,4,128,128]{3,2,1,0:T(8,128)S(1)} %bitcast.32, f32[1,4,128,128]{3,2,1,0:T(8,128)S(1)} %bitcast.26, f32[1,4,128,128]{3,2,1,0:T(8,128)S(1)} %bitcast.31, f32[1,4,128,128]{3,2,1,0:T(8,128)} %bitcast.15), kind=kLoop, calls=%fused_computation.6 | loop fusion | flops 786432 | bytes 2097152 | tf_op jit(solution)/shard_map/stack | solution.py:308
  99.2 17.6 %shard_map.60 = f32[1024,2048]{1,0:T(8,128)} custom-call(s32[6]{0:T(128)} %stack.72.sp_ref, bf16[1024,2048]{1,0:T(8,128)(2,1)} %q_ref.9, f32[16,1024,10]{2,1,0:T(8,128)} %bitcast.23, f32[1024,2048]{1,0:T(8,128)} %shard_map.58.l_ref, f32[16,128,128]{2,1,0:T(8,128)} %pad_maximum_fusion.rest_0_, ...), custom_call_target="tpu_custom_call", output_to_operand_aliasing={{}: (3, {})} | custom-call | flops 2684354560 | bytes 20971520 | tf_op jit(solution)/shard_map/pallas_call | solution.py:190
  (14 shorter events, 0.0 us)
Async XLA Ops:
  6.5 2.0 %collective-permute-start = (f32[8,128,128]{2,1,0:T(8,128)S(1)}, f32[8,128,128]{2,1,0:T(8,128)S(1)}, u32[]{:S(2)}, u32[]{:S(2)}) collective-permute-start(f32[8,128,128]{2,1,0:T(8,128)S(1)} %get-tuple-element.9), channel_id=1, source_target_pairs={{0,1},{1,0},{2,3},{3,2},{4,5},{5,4},{6,7},{7,6},{8,9},{9,8},{10,11... | collective-permute-start | bytes 1572872 | tf_op jit(solution)/shard_map/ppermute | solution.py:218
  9.6 14.3 %collective-permute-start.2 = (f32[8,128,128]{2,1,0:T(8,128)S(1)}, f32[8,128,128]{2,1,0:T(8,128)S(1)}, u32[]{:S(2)}, u32[]{:S(2)}) collective-permute-start(f32[8,128,128]{2,1,0:T(8,128)S(1)} %dynamic-slice_add_fusion), channel_id=1, source_target_pairs={{0,2},{2,0},{1,3},{3,1},{4,6},{6,4},{5,7},{7,5},{8,10},{10,8},{9,1... | collective-permute-start | bytes 1572872 | tf_op jit(solution)/shard_map/ppermute | solution.py:218
  12.0 12.9 %collective-permute-start.1 = (f32[8,128,128]{2,1,0:T(8,128)S(1)}, f32[8,128,128]{2,1,0:T(8,128)S(1)}, u32[]{:S(2)}, u32[]{:S(2)}) collective-permute-start(f32[8,128,128]{2,1,0:T(8,128)S(1)} %get-tuple-element.10), channel_id=1, source_target_pairs={{0,1},{1,0},{2,3},{3,2},{4,5},{5,4},{6,7},{7,6},{8,9},{9,8},{10,11... | collective-permute-start | bytes 1572872 | tf_op jit(solution)/shard_map/ppermute | solution.py:218
  23.9 5.3 %copy-start.2 = (f32[8,128,128]{2,1,0:T(8,128)}, f32[8,128,128]{2,1,0:T(8,128)S(1)}, u32[]{:S(2)}) copy-start(f32[8,128,128]{2,1,0:T(8,128)S(1)} %collective-permute-done.2) | copy-start | bytes 1572868
  23.9 2.5 %collective-permute-start.3 = (f32[8,128,128]{2,1,0:T(8,128)S(1)}, f32[8,128,128]{2,1,0:T(8,128)S(1)}, u32[]{:S(2)}, u32[]{:S(2)}) collective-permute-start(f32[8,128,128]{2,1,0:T(8,128)S(1)} %collective-permute-done.2), channel_id=1, source_target_pairs={{0,1},{1,0},{2,3},{3,2},{4,5},{5,4},{6,7},{7,6},{8,9},{9,8},{10,11... | collective-permute-start | bytes 1572872 | tf_op jit(solution)/shard_map/ppermute | solution.py:218
  25.0 1.4 %copy-start = (f32[8,128,128]{2,1,0:T(8,128)}, f32[8,128,128]{2,1,0:T(8,128)S(1)}, u32[]{:S(2)}) copy-start(f32[8,128,128]{2,1,0:T(8,128)S(1)} %get-tuple-element.7) | copy-start | bytes 1572868
  25.0 2.6 %copy-start.1 = (f32[8,128,128]{2,1,0:T(8,128)}, f32[8,128,128]{2,1,0:T(8,128)S(1)}, u32[]{:S(2)}) copy-start(f32[8,128,128]{2,1,0:T(8,128)S(1)} %get-tuple-element.8) | copy-start | bytes 1572868
  26.4 8.7 %copy-start.3 = (f32[8,128,128]{2,1,0:T(8,128)}, f32[8,128,128]{2,1,0:T(8,128)S(1)}, u32[]{:S(2)}) copy-start(f32[8,128,128]{2,1,0:T(8,128)S(1)} %collective-permute-done.3) | copy-start | bytes 1572868
  27.6 7.6 %collective-permute-start.4 = (f32[4,128,128]{2,1,0:T(8,128)S(1)}, f32[4,128,128]{2,1,0:T(8,128)S(1)}, u32[]{:S(2)}, u32[]{:S(2)}) collective-permute-start(f32[4,128,128]{2,1,0:T(8,128)S(1)} %fusion.2), channel_id=1, source_target_pairs={{0,4},{4,0},{8,12},{12,8},{16,20},{20,16},{24,28},{28,24},{1,5},{5... | collective-permute-start | bytes 786440 | tf_op jit(solution)/shard_map/ppermute | solution.py:218
  35.2 0.8 copy-start.4
  36.0 24.4 %collective-permute-start.8 = (f32[4,128,128]{2,1,0:T(8,128)}, f32[4,128,128]{2,1,0:T(8,128)}, u32[]{:S(2)}, u32[]{:S(2)}) collective-permute-start(f32[4,128,128]{2,1,0:T(8,128)} %add.42), channel_id=1, source_target_pairs={{0,8},{8,0},{4,12},{12,4},{16,24},{24,16},{20,28},{28,20},{1,9},{9... | collective-permute-start | bytes 786440 | tf_op jit(solution)/shard_map/ppermute | solution.py:218
  59.2 19.5 %collective-permute-start.6 = (f32[4,128,128]{2,1,0:T(8,128)}, f32[4,128,128]{2,1,0:T(8,128)}, u32[]{:S(2)}, u32[]{:S(2)}) collective-permute-start(f32[4,128,128]{2,1,0:T(8,128)} %copy-done.4), channel_id=1, source_target_pairs={{0,2},{1,3},{2,0},{3,1},{4,6},{5,7},{6,4},{7,5},{8,10},{9,11},{10,... | collective-permute-start | bytes 786440 | tf_op jit(solution)/shard_map/ppermute | solution.py:223
  62.1 16.8 %collective-permute-start.12 = (f32[4,128,128]{2,1,0:T(8,128)}, f32[4,128,128]{2,1,0:T(8,128)}, u32[]{:S(2)}, u32[]{:S(2)}) collective-permute-start(f32[4,128,128]{2,1,0:T(8,128)} %add.43), channel_id=1, source_target_pairs={{0,16},{4,20},{8,24},{12,28},{1,17},{5,21},{9,25},{13,29},{2,18},{... | collective-permute-start | bytes 786440 | tf_op jit(solution)/shard_map/ppermute | solution.py:218
  76.4 12.5 %collective-permute-start.5 = (f32[4,128,128]{2,1,0:T(8,128)}, f32[4,128,128]{2,1,0:T(8,128)S(1)}, u32[]{:S(2)}, u32[]{:S(2)}) collective-permute-start(f32[4,128,128]{2,1,0:T(8,128)} %copy-done.4), channel_id=1, source_target_pairs={{0,1},{1,0},{2,3},{3,2},{4,5},{5,4},{6,7},{7,6},{8,9},{9,8},{10,11... | collective-permute-start | bytes 786440 | tf_op jit(solution)/shard_map/ppermute | solution.py:223
  78.4 8.1 %collective-permute-start.10 = (f32[4,128,128]{2,1,0:T(8,128)}, f32[4,128,128]{2,1,0:T(8,128)S(1)}, u32[]{:S(2)}, u32[]{:S(2)}) collective-permute-start(f32[4,128,128]{2,1,0:T(8,128)} %collective-permute-done.8), channel_id=1, source_target_pairs={{0,2},{1,3},{2,0},{3,1},{4,6},{5,7},{6,4},{7,5},{8,10},{9,11},{10,... | collective-permute-start | bytes 786440 | tf_op jit(solution)/shard_map/ppermute | solution.py:223
  78.7 14.3 %collective-permute-start.7 = (f32[4,128,128]{2,1,0:T(8,128)}, f32[4,128,128]{2,1,0:T(8,128)S(1)}, u32[]{:S(2)}, u32[]{:S(2)}) collective-permute-start(f32[4,128,128]{2,1,0:T(8,128)} %collective-permute-done.6), channel_id=1, source_target_pairs={{0,1},{1,0},{2,3},{3,2},{4,5},{5,4},{6,7},{7,6},{8,9},{9,8},{10,11... | collective-permute-start | bytes 786440 | tf_op jit(solution)/shard_map/ppermute | solution.py:223
  79.0 13.1 %collective-permute-start.14 = (f32[4,128,128]{2,1,0:T(8,128)}, f32[4,128,128]{2,1,0:T(8,128)S(1)}, u32[]{:S(2)}, u32[]{:S(2)}) collective-permute-start(f32[4,128,128]{2,1,0:T(8,128)} %collective-permute-done.12), channel_id=1, source_target_pairs={{0,2},{1,3},{2,0},{3,1},{4,6},{5,7},{6,4},{7,5},{8,10},{9,11},{10,... | collective-permute-start | bytes 786440 | tf_op jit(solution)/shard_map/ppermute | solution.py:223
  81.5 13.6 %collective-permute-start.9 = (f32[4,128,128]{2,1,0:T(8,128)}, f32[4,128,128]{2,1,0:T(8,128)S(1)}, u32[]{:S(2)}, u32[]{:S(2)}) collective-permute-start(f32[4,128,128]{2,1,0:T(8,128)} %collective-permute-done.8), channel_id=1, source_target_pairs={{0,1},{1,0},{2,3},{3,2},{4,5},{5,4},{6,7},{7,6},{8,9},{9,8},{10,11... | collective-permute-start | bytes 786440 | tf_op jit(solution)/shard_map/ppermute | solution.py:223
  86.5 8.6 %collective-permute-start.11 = (f32[4,128,128]{2,1,0:T(8,128)S(1)}, f32[4,128,128]{2,1,0:T(8,128)S(1)}, u32[]{:S(2)}, u32[]{:S(2)}) collective-permute-start(f32[4,128,128]{2,1,0:T(8,128)S(1)} %collective-permute-done.10), channel_id=1, source_target_pairs={{0,1},{1,0},{2,3},{3,2},{4,5},{5,4},{6,7},{7,6},{8,9},{9,8},{10,11... | collective-permute-start | bytes 786440 | tf_op jit(solution)/shard_map/ppermute | solution.py:223
  88.9 8.2 %collective-permute-start.13 = (f32[4,128,128]{2,1,0:T(8,128)}, f32[4,128,128]{2,1,0:T(8,128)S(1)}, u32[]{:S(2)}, u32[]{:S(2)}) collective-permute-start(f32[4,128,128]{2,1,0:T(8,128)} %collective-permute-done.12), channel_id=1, source_target_pairs={{0,1},{1,0},{2,3},{3,2},{4,5},{5,4},{6,7},{7,6},{8,9},{9,8},{10,11... | collective-permute-start | bytes 786440 | tf_op jit(solution)/shard_map/ppermute | solution.py:223
  92.1 5.0 %collective-permute-start.15 = (f32[4,128,128]{2,1,0:T(8,128)S(1)}, f32[4,128,128]{2,1,0:T(8,128)S(1)}, u32[]{:S(2)}, u32[]{:S(2)}) collective-permute-start(f32[4,128,128]{2,1,0:T(8,128)S(1)} %collective-permute-done.14), channel_id=1, source_target_pairs={{0,1},{1,0},{2,3},{3,2},{4,5},{5,4},{6,7},{7,6},{8,9},{9,8},{10,11... | collective-permute-start | bytes 786440 | tf_op jit(solution)/shard_map/ppermute | solution.py:223
